TPU v7x, 128 devices: a whole 4x4x4 slice. The times are simulated.
128 devices in a mesh: gx: 16 (over z, y_hi, core), gy: 8 (over y_lo, x).
Axes of the slice: x: 4, y: 4 (y_hi: 2, y_lo: 2; y = y_hi * 2 + y_lo), z: 4, core: 2. Of those that a mesh axis runs over, the one named last changes fastest.
Arguments:
- velocity: float32 [3, 128, 64, 256], P(None, 'gy', 'gx'), may hold values from -6 to 6
- point_velocity: float32 [3, 16384], P(None, ('gx', 'gy')), may hold values from -8 to 8
- point_coef: float32 [16384], P(('gx', 'gy')), may hold values from 0.05 to 0.5
- point_width: float32 [16384], P(('gx', 'gy')), may hold values from 0.8 to 2
- send_point: int32 [128, 2048], P(('gx', 'gy')), may hold values from 0 to 127
- send_count: int32 [128, 128], P(('gx', 'gy')), may hold values from 0 to 16, as said below
- slot_offset: float32 [3, 128, 2048], P(None, ('gx', 'gy')), may hold values from 0.5 to 3.5
- send_anchor: int32 [128, 2048], P(('gx', 'gy')), may hold values from 0 to 12540, as said below
- vertical_inverse: float32 [64, 64], replicated, may hold values from -1 to 2, as said below
Outputs:
- new_velocity: float32 [3, 128, 64, 256], P(None, 'gy', 'gx')
Inputs may be any that keep to these rules, and one draw needn't show every extreme that they name: `send_count`: one destination tile, drawn from the seed, has 16 records from every source device. `send_anchor`: every block of 4 x 4 x 4 cells at the corner lies inside the destination tile: the corner is x * 4 * 256 + z * 256 + y with x <= 12, z <= 0, y <= 252. `vertical_inverse`: a dense matrix.
All inputs are finite; a program needn't handle non-finite values.
Results may differ from a plain program's by a relative error of at most 0.00007.
Values sent between devices are 32-bit elements; how exact they have to be, the bound alone decides.
No kernel may reach another device: no remote copies, remote signals or barrier semaphores. Data moves between devices by JAX's collectives and lax.ppermute only.
A program may use at most 64 MiB of HBM per device.

v0:
```python
import math

import jax
import jax.numpy as jnp
from jax import lax
from jax.experimental import pallas as pl
from jax.sharding import PartitionSpec as P


def _rows(pieces, shape):
    row = lax.broadcasted_iota(jnp.int32, shape, 0)
    total = jnp.zeros(shape, jnp.float32)
    for k, piece in enumerate(pieces):
        total = jnp.where(row == k, jnp.broadcast_to(piece, shape), total)
    return total


def _pieces(x):
    high = x.astype(jnp.bfloat16)
    rest = x - high.astype(jnp.float32)
    middle = rest.astype(jnp.bfloat16)
    low = (rest - middle.astype(jnp.float32)).astype(jnp.bfloat16)
    return high, middle, low


def _exact_dot(values, pick, dims):
    total = None
    for piece in _pieces(values):
        term = lax.dot_general(piece, pick, dims, preferred_element_type=jnp.float32)
        total = term if total is None else total + term
    return total


def _exact_dot_picked_right(pick, values, dims):
    total = None
    for piece in _pieces(values):
        term = lax.dot_general(pick, piece, dims, preferred_element_type=jnp.float32)
        total = term if total is None else total + term
    return total


def source_kernel(pv_ref, coef_ref, width_ref, sp_ref, cnt_ref, off_ref, out_ref):
    points = pv_ref.shape[1]
    slots = sp_ref.shape[1]
    tiles = cnt_ref.shape[1]
    capacity = slots // tiles
    lanes_out = out_ref.shape[1]
    fields = lanes_out // capacity
    plain = (((1,), (0,)), ((), ()))
    pv = pv_ref[...]
    speed = jnp.sqrt(pv[0:1] * pv[0:1] + pv[1:2] * pv[1:2] + pv[2:3] * pv[2:3])
    force = -(coef_ref[...] * speed) * pv
    vals = _rows([force[0:1], force[1:2], force[2:3], width_ref[...]], (8, points))
    pick = (lax.broadcasted_iota(jnp.int32, (points, slots), 0) == sp_ref[...]).astype(jnp.bfloat16)
    picked = _exact_dot(vals, pick, plain)
    slot_at = lax.broadcasted_iota(jnp.int32, (tiles, slots), 1)
    tile_at = lax.broadcasted_iota(jnp.int32, (tiles, slots), 0)
    tile_of = (slot_at // capacity == tile_at).astype(jnp.bfloat16)
    counts = _rows([cnt_ref[...].astype(jnp.float32)], (8, tiles)).astype(jnp.bfloat16)
    limit = lax.dot_general(counts, tile_of, plain, preferred_element_type=jnp.float32)[0:1]
    lane = (lax.broadcasted_iota(jnp.int32, (1, slots), 1) % capacity).astype(jnp.float32)
    live = jnp.where(lane < limit, 1.0, 0.0)
    table = _rows([picked[0:1] * live, picked[1:2] * live, picked[2:3] * live,
                   off_ref[0, 0:1, :], off_ref[1, 0:1, :], off_ref[2, 0:1, :], picked[3:4]],
                  (fields, slots))
    spread = jnp.concatenate(
        [jnp.broadcast_to(table[v:v + 1], (capacity, slots)) for v in range(fields)], axis=0)
    same_c = (lax.broadcasted_iota(jnp.int32, (lanes_out, slots), 1) % capacity
              == lax.broadcasted_iota(jnp.int32, (lanes_out, slots), 0) % capacity)
    spread = jnp.where(same_c, spread, 0.0)
    out_ref[...] = _exact_dot_picked_right(tile_of, spread, (((1,), (1,)), ((), ())))


def source_records(pv, coef, width, sp, cnt, off):
    tiles = cnt.shape[1]
    capacity = sp.shape[1] // tiles
    return pl.pallas_call(
        source_kernel,
        out_shape=jax.ShapeDtypeStruct((tiles, 8 * capacity), jnp.float32),
    )(pv, coef, width, sp, cnt, off)


K = 4


time_step = 0.25


def with_halo(block, sides, width, periodic):
    for axis, dim in sides:
        count = lax.axis_size(axis)
        forward = [(i, i + 1) for i in range(count - 1)]
        if periodic:
            forward.append((count - 1, 0))
        backward = [(target, source) for source, target in forward]
        low = lax.ppermute(
            lax.slice_in_dim(block, block.shape[dim] - width, None, axis=dim), axis, forward
        )
        high = lax.ppermute(lax.slice_in_dim(block, 0, width, axis=dim), axis, backward)
        block = jnp.concatenate([low, block, high], axis=dim)
    return block


def block_factor(corner, offset, extent, inverse_square, block_edge):
    cells = jnp.arange(extent, dtype=jnp.int32)[:, None]
    shifted = cells - corner[None, :]
    inside = (shifted >= 0) & (shifted < block_edge)
    spread = shifted.astype(jnp.float32) + 0.5 - offset[None, :]
    return jnp.where(inside, jnp.exp(-(spread * spread) * inverse_square[None, :]), 0.0)


def deposit_blocks(arrived, corner_x, corner_z, corner_y, rows_x, rows_z, rows_y, block_edge):
    width = arrived[6]
    inverse_square = 1.0 / (width * width)
    scaled = arrived[0:3] / (math.pi**1.5 * width**3)[None, :]
    along_x = block_factor(corner_x, arrived[3], rows_x, inverse_square, block_edge)
    along_z = block_factor(corner_z, arrived[4], rows_z, inverse_square, block_edge)
    along_y = block_factor(corner_y, arrived[5], rows_y, inverse_square, block_edge)
    left = scaled[:, None, None, :] * along_x[None, :, None, :] * along_z[None, None, :, :]
    left = left.reshape(3 * rows_x * rows_z, -1)
    result = lax.dot_general(
        left,
        along_y,
        (((1,), (1,)), ((), ())),
        precision=lax.Precision.HIGH,
        preferred_element_type=jnp.float32,
    )
    return result.reshape(3, rows_x, rows_z, rows_y)


def local(
    velocity,
    point_velocity,
    point_coef,
    point_width,
    send_point,
    send_count,
    slot_offset,
    send_anchor,
    vertical_inverse,
):
    rows_x = velocity.shape[1]
    rows_z = velocity.shape[2]
    rows_y = velocity.shape[3]
    slot_total = send_point.shape[1]
    device_count = lax.axis_size("gx") * lax.axis_size("gy")
    capacity = slot_total // device_count
    records = source_records(
        point_velocity,
        point_coef[None, :],
        point_width[None, :],
        send_point,
        send_count,
        slot_offset,
    )
    fields = records.shape[1] // capacity
    arrived = lax.all_to_all(records, ("gx", "gy"), split_axis=0, concat_axis=0, tiled=True)
    arrived = arrived.reshape(device_count, fields, capacity).transpose(1, 0, 2)
    arrived = arrived.reshape(fields, slot_total)
    anchors = send_anchor[0]
    corner_x = anchors // (rows_z * rows_y)
    remainder = anchors % (rows_z * rows_y)
    corner_z = remainder // rows_y
    corner_y = remainder % rows_y
    forcing = deposit_blocks(arrived, corner_x, corner_z, corner_y, rows_x, rows_z, rows_y, K)
    wide_x = with_halo(velocity, (("gy", 1),), 1, True)
    grad_x = (wide_x[:, 2:] - wide_x[:, :-2]) * 0.5
    grad_y = (jnp.roll(velocity, -1, axis=3) - jnp.roll(velocity, 1, axis=3)) * 0.5
    flat_part = velocity[0:1] * grad_x + velocity[1:2] * grad_y
    partial = velocity + time_step * (forcing - flat_part)
    both = jnp.concatenate([velocity, partial], axis=0)
    columns = lax.all_to_all(both, "gx", split_axis=1, concat_axis=2, tiled=True)
    column_velocity = columns[0:3]
    padded = jnp.pad(column_velocity, ((0, 0), (0, 0), (1, 1), (0, 0)))
    grad_z = (padded[:, :, 2:] - padded[:, :, :-2]) * 0.5
    columns = columns[3:6] - time_step * (column_velocity[2:3] * grad_z)
    solved = jnp.einsum("zk,cxky->cxzy", vertical_inverse, columns, precision=lax.Precision.HIGHEST)
    solved = solved.reshape(3, rows_x, rows_z, rows_y)
    new_velocity = lax.all_to_all(solved, "gx", split_axis=1, concat_axis=1, tiled=True)
    return new_velocity


def solution(mesh):
    placed = (
        P(None, "gy", "gx", None),
        P(None, ("gx", "gy")),
        P(("gx", "gy")),
        P(("gx", "gy")),
        P(("gx", "gy"), None),
        P(("gx", "gy"), None),
        P(None, ("gx", "gy"), None),
        P(("gx", "gy"), None),
        P(),
    )

    return jax.shard_map(
        local, mesh=mesh, in_specs=placed, out_specs=P(None, "gy", "gx", None), check_vma=False
    )
```

profile of v0, /device:TPU:1, one launch (start us, length us, event | category | flops | bytes accessed | tf_op | source)
XLA Modules:
  0.0 57.3 jit_solution(3704850093480636255)
XLA Ops:
  0.0 0.8 %fusion.63 = (f32[3,1,4,256]{3,2,1,0:T(4,128)S(1)}, f32[3,1,4,256]{3,2,1,0:T(4,128)S(1)}) fusion(f32[3,16,4,256]{3,2,1,0:T(4,128)} %param.9), kind=kLoop, calls=%fused_computation.85 | loop fusion | bytes 49152 | tf_op jit(solution)/shard_map/slice | solution.py:99
  0.8 2.1 %collective-permute-start.1 = (f32[3,1,4,256]{3,1,2,0:T(1,128)S(1)}, f32[3,1,4,256]{3,1,2,0:T(1,128)S(1)}, u32[]{:S(2)}, u32[]{:S(2)}) collective-permute-start(f32[3,1,4,256]{3,1,2,0:T(1,128)S(1)} %copy.52), channel_id=1, source_target_pairs={{0,1},{1,2},{2,3},{3,4},{4,5},{5,6},{6,7},{7,0},{8,9},{9,10},{10,1... | collective-permute-start | bytes 36872 | tf_op jit(solution)/shard_map/ppermute | solution.py:96
  2.9 2.4 %collective-permute-start = (f32[3,1,4,256]{3,1,2,0:T(1,128)S(1)}, f32[3,1,4,256]{3,1,2,0:T(1,128)S(1)}, u32[]{:S(2)}, u32[]{:S(2)}) collective-permute-start(f32[3,1,4,256]{3,1,2,0:T(1,128)S(1)} %copy.50), channel_id=1, source_target_pairs={{1,0},{2,1},{3,2},{4,3},{5,4},{6,5},{7,6},{0,7},{9,8},{10,9},{11,1... | collective-permute-start | bytes 36872 | tf_op jit(solution)/shard_map/ppermute | solution.py:99
  5.3 2.5 %shard_map.91 = f32[128,128]{1,0:T(8,128)} custom-call(f32[3,128]{1,0:T(4,128)} %pv_ref.1, f32[1,128]{1,0:T(1,128)} %bitcast.52, f32[1,128]{1,0:T(1,128)} %bitcast.53, s32[1,2048]{1,0:T(1,128)} %sp_ref.1, s32[1,128]{1,0:T(1,128)} %cnt_ref.1, f32[3,1,2048]{2,1,0:T(1,128)} %off_ref.1), custom_call_target="tpu_custom_call" | custom-call | tf_op jit(solution)/shard_map/pallas_call | solution.py:77
  7.8 9.2 %all-to-all-start = ((f32[128,1,128]{2,1,0:T(1,128)}), f32[128,1,128]{2,1,0:T(1,128)S(1)}, u32[]{:S(2)}, u32[]{:S(2)}) async-start(f32[128,1,128]{2,1,0:T(1,128)} %bitcast.46), calls=%async_computation | async-start | bytes 131072 | tf_op jit(solution)/shard_map/all_to_all | solution.py:157
  17.0 0.1 fusion.61
  17.1 0.0 copy-start.2
  17.1 0.1 fusion.62
  17.2 0.6 %copy-done.2 = s32[1,2048]{1,0:T(1,128)S(1)} copy-done((s32[1,2048]{1,0:T(1,128)S(1)}, s32[1,2048]{1,0:T(1,128)}, u32[]{:S(2)}) %copy-start.2) | copy-done | bytes 8216
  17.8 0.1 and_select_fusion.1
  18.0 8.8 %all-to-all-done = f32[128,1,128]{2,1,0:T(1,128)S(1)} async-done(((f32[128,1,128]{2,1,0:T(1,128)}), f32[128,1,128]{2,1,0:T(1,128)S(1)}, u32[]{:S(2)}, u32[]{:S(2)}) %all-to-all-start) | async-done | bytes 65568 | tf_op jit(solution)/shard_map/all_to_all | solution.py:157
  26.8 0.1 copy.44
  26.9 0.1 copy.47
  27.0 0.1 sub.119
  27.1 0.1 copy.48
  27.2 0.1 sub.126
  27.3 0.1 copy.46
  27.4 0.1 squeeze.4
  27.5 0.1 copy.45
  27.6 0.1 slice.83
  27.8 0.1 exponential_select_fusion
  27.9 0.1 copy.49
  28.0 0.1 sub.133
  28.1 2.1 %fusion.36 = f32[3,16,4,256]{3,1,2,0:T(8,128)S(1)} fusion(f32[3,16,4,256]{3,1,2,0:T(8,128)S(1)} %copy.63, f32[3,1,4,256]{3,1,2,0:T(1,128)S(1)} %collective-permute-done.1, f32[3,1,4,256]{3,1,2,0:T(1,128)S(1)} %collective-permute-done, f32[3,16,4,1]{3,1,2,0:T(8,128)S(1)} %get-tuple-element.14, f32[3,16,4,255]{3,1,2,0:T(8,128)S(1)} %get-tuple-element.16, ...), kind=kOutput, calls=%fused_computation.39 | convolution fusion | flops 610729984 | bytes 1392640 | tf_op jit(solution)/shard_map/dot_general | solution.py:121
  30.2 0.3 copy.64
  30.5 13.5 %all_to_all.23 = f32[6,16,4,256]{3,2,0,1:T(4,128)S(1)} all-to-all(f32[6,16,4,256]{3,2,0,1:T(4,128)S(1)} %copy.64), channel_id=1, replica_groups=mesh['gx'=16,'gy'=8] {'gx'}, dimensions={1} | all-to-all | bytes 786432 | tf_op jit(solution)/shard_map/all_to_all | solution.py:172
  44.1 0.1 slice.101
  44.2 0.1 slice.99
  44.3 0.4 convolution_bitcast_fusion
  44.6 0.1 reshape.209
  44.7 11.9 %all_to_all.24 = f32[3,16,4,256]{3,2,0,1:T(4,128)S(1)} all-to-all(f32[3,16,4,256]{3,2,0,1:T(4,128)S(1)} %copy.67), channel_id=1, replica_groups=mesh['gx'=16,'gy'=8] {'gx'}, dimensions={1} | all-to-all | bytes 393216 | tf_op jit(solution)/shard_map/all_to_all | solution.py:179
  56.6 0.7 %copy.68 = f32[3,16,4,256]{3,2,1,0:T(4,128)} copy(f32[3,16,4,256]{3,2,0,1:T(4,128)S(1)} %all_to_all.24) | data formatting | bytes 393216 | tf_op jit(solution)/shard_map/all_to_all | solution.py:179
  (27 shorter events, 0.4 us)
Async XLA Ops:
  0.0 44.2 %copy-start = (f32[64,64]{1,0:T(8,128)S(1)}, f32[64,64]{1,0:T(8,128)}, u32[]{:S(2)}) copy-start(f32[64,64]{1,0:T(8,128)} %param.17) | copy-start | bytes 49156
  0.0 17.0 %copy-start.1 = (f32[3,16,4,256]{3,2,1,0:T(4,128)S(1)}, f32[3,16,4,256]{3,2,1,0:T(4,128)}, u32[]{:S(2)}) copy-start(f32[3,16,4,256]{3,2,1,0:T(4,128)} %param.9) | copy-start | bytes 589828
  0.8 27.3 %collective-permute-start.1 = (f32[3,1,4,256]{3,1,2,0:T(1,128)S(1)}, f32[3,1,4,256]{3,1,2,0:T(1,128)S(1)}, u32[]{:S(2)}, u32[]{:S(2)}) collective-permute-start(f32[3,1,4,256]{3,1,2,0:T(1,128)S(1)} %copy.52), channel_id=1, source_target_pairs={{0,1},{1,2},{2,3},{3,4},{4,5},{5,6},{6,7},{7,0},{8,9},{9,10},{10,1... | collective-permute-start | bytes 36872 | tf_op jit(solution)/shard_map/ppermute | solution.py:96
  2.9 25.2 %collective-permute-start = (f32[3,1,4,256]{3,1,2,0:T(1,128)S(1)}, f32[3,1,4,256]{3,1,2,0:T(1,128)S(1)}, u32[]{:S(2)}, u32[]{:S(2)}) collective-permute-start(f32[3,1,4,256]{3,1,2,0:T(1,128)S(1)} %copy.50), channel_id=1, source_target_pairs={{1,0},{2,1},{3,2},{4,3},{5,4},{6,5},{7,6},{0,7},{9,8},{10,9},{11,1... | collective-permute-start | bytes 36872 | tf_op jit(solution)/shard_map/ppermute | solution.py:99
  7.8 19.0 %all-to-all-start = ((f32[128,1,128]{2,1,0:T(1,128)}), f32[128,1,128]{2,1,0:T(1,128)S(1)}, u32[]{:S(2)}, u32[]{:S(2)}) async-start(f32[128,1,128]{2,1,0:T(1,128)} %bitcast.46), calls=%async_computation | async-start | bytes 131072 | tf_op jit(solution)/shard_map/all_to_all | solution.py:157
  17.1 0.7 %copy-start.2 = (s32[1,2048]{1,0:T(1,128)S(1)}, s32[1,2048]{1,0:T(1,128)}, u32[]{:S(2)}) copy-start(s32[1,2048]{1,0:T(1,128)} %param.16) | copy-start | bytes 24580
where the time goes:
time: 57.6 us; the launch traced here: 57.3 us
  blocking collectives  25.3 us (44%)
  starting transfers between devices  13.6 us (24%)
  waiting for transfers between devices  8.76 us (15%)
  local copies, waits for them, and re-layouts  3.99 us (7%)
  Pallas kernels  2.47 us (4%)
  matrix products  2.42 us (4%)
    all_to_all x1, blocking collectives, local(): lax.all_to_all(both, 'gx', split_axis=1, concat_axis=2, tiled=True)  13.5 us
    all_to_all x1, blocking collectives, local(): lax.all_to_all(solved, 'gx', split_axis=1, concat_axis=1, tiled=True)  11.9 us
    all_to_all x1, starting transfers between devices, local(): lax.all_to_all(records, ('gx', 'gy'), split_axis=0, concat_axis=0, tiled=...  9.18 us
    all_to_all x1, waiting for transfers between devices, local(): lax.all_to_all(records, ('gx', 'gy'), split_axis=0, concat_axis=0, tiled=...  8.75 us
    pallas_call x1, Pallas kernels, source_records(): pl.pallas_call(source_kernel, out_shape=jax.ShapeDtypeStruct((tiles, 8 *...  2.47 us
    ppermute x1, starting transfers between devices, with_halo(): lax.ppermute(lax.slice_in_dim(block, 0, width, axis=dim), axis, backward)  2.37 us
    ppermute x1, starting transfers between devices, with_halo(): lax.ppermute(lax.slice_in_dim(block, block.shape[dim] - width, None, axis...  2.1 us
    dot_general x1, matrix products, deposit_blocks(): lax.dot_general(left, along_y, (((1,), (1,)), ((), ())), precision=lax.Pr...  2.06 us
  transfers between devices with their start and end apart: 3, of which 1 were waited for; matrix products, arithmetic and copies ran while one was open for 3% of the time, Pallas kernels for 4%

commit v1 on v0

--- a/solution.py
+++ b/solution.py
@@ -31,14 +31,6 @@
     return total
 
 
-def _exact_dot_picked_right(pick, values, dims):
-    total = None
-    for piece in _pieces(values):
-        term = lax.dot_general(pick, piece, dims, preferred_element_type=jnp.float32)
-        total = term if total is None else total + term
-    return total
-
-
 def source_kernel(pv_ref, coef_ref, width_ref, sp_ref, cnt_ref, off_ref, out_ref):
     points = pv_ref.shape[1]
     slots = sp_ref.shape[1]
@@ -68,7 +60,10 @@
     same_c = (lax.broadcasted_iota(jnp.int32, (lanes_out, slots), 1) % capacity
               == lax.broadcasted_iota(jnp.int32, (lanes_out, slots), 0) % capacity)
     spread = jnp.where(same_c, spread, 0.0)
-    out_ref[...] = _exact_dot_picked_right(tile_of, spread, (((1,), (1,)), ((), ())))
+    slot_row = lax.broadcasted_iota(jnp.int32, (slots, tiles), 0)
+    tile_col = lax.broadcasted_iota(jnp.int32, (slots, tiles), 1)
+    slot_tile = (slot_row // capacity == tile_col).astype(jnp.bfloat16)
+    out_ref[...] = _exact_dot(spread, slot_tile, plain).T
 
 
 def source_records(pv, coef, width, sp, cnt, off):

time: 57.6 us -> 57.8 us (level)
  transfers between devices with their start and end apart: 3 -> 3, of which waited for: 1 -> 1; matrix products, arithmetic and copies ran while one was open for 3% -> 3% of each run, Pallas kernels for 4% -> 5%
where the time goes in v1:
time: 57.8 us; the launch traced here: 57.5 us
  blocking collectives  25.3 us (44%)
  starting transfers between devices  13.6 us (24%)
  waiting for transfers between devices  8.76 us (15%)
  local copies, waits for them, and re-layouts  3.99 us (7%)
  Pallas kernels  2.65 us (5%)
  matrix products  2.42 us (4%)
    all_to_all x1, blocking collectives, local(): lax.all_to_all(both, 'gx', split_axis=1, concat_axis=2, tiled=True)  13.5 us
    all_to_all x1, blocking collectives, local(): lax.all_to_all(solved, 'gx', split_axis=1, concat_axis=1, tiled=True)  11.9 us
    all_to_all x1, starting transfers between devices, local(): lax.all_to_all(records, ('gx', 'gy'), split_axis=0, concat_axis=0, tiled=...  9.18 us
    all_to_all x1, waiting for transfers between devices, local(): lax.all_to_all(records, ('gx', 'gy'), split_axis=0, concat_axis=0, tiled=...  8.75 us
    pallas_call x1, Pallas kernels, source_records(): pl.pallas_call(source_kernel, out_shape=jax.ShapeDtypeStruct((tiles, 8 *...  2.65 us
    ppermute x1, starting transfers between devices, with_halo(): lax.ppermute(lax.slice_in_dim(block, 0, width, axis=dim), axis, backward)  2.37 us
    ppermute x1, starting transfers between devices, with_halo(): lax.ppermute(lax.slice_in_dim(block, block.shape[dim] - width, None, axis...  2.1 us
    dot_general x1, matrix products, deposit_blocks(): lax.dot_general(left, along_y, (((1,), (1,)), ((), ())), precision=lax.Pr...  2.06 us
  transfers between devices with their start and end apart: 3, of which 1 were waited for; matrix products, arithmetic and copies ran while one was open for 3% of the time, Pallas kernels for 5%

profile of v1, /device:TPU:1, one launch (start us, length us, event | category | flops | bytes accessed | tf_op | source)
XLA Modules:
  0.0 57.5 jit_solution(3248877844551798238)
XLA Ops:
  0.0 0.8 %fusion.63 = (f32[3,1,4,256]{3,2,1,0:T(4,128)S(1)}, f32[3,1,4,256]{3,2,1,0:T(4,128)S(1)}) fusion(f32[3,16,4,256]{3,2,1,0:T(4,128)} %param.9), kind=kLoop, calls=%fused_computation.85 | loop fusion | bytes 49152 | tf_op jit(solution)/shard_map/slice | solution.py:94
  0.8 2.1 %collective-permute-start.1 = (f32[3,1,4,256]{3,1,2,0:T(1,128)S(1)}, f32[3,1,4,256]{3,1,2,0:T(1,128)S(1)}, u32[]{:S(2)}, u32[]{:S(2)}) collective-permute-start(f32[3,1,4,256]{3,1,2,0:T(1,128)S(1)} %copy.52), channel_id=1, source_target_pairs={{0,1},{1,2},{2,3},{3,4},{4,5},{5,6},{6,7},{7,0},{8,9},{9,10},{10,1... | collective-permute-start | bytes 36872 | tf_op jit(solution)/shard_map/ppermute | solution.py:91
  2.9 2.4 %collective-permute-start = (f32[3,1,4,256]{3,1,2,0:T(1,128)S(1)}, f32[3,1,4,256]{3,1,2,0:T(1,128)S(1)}, u32[]{:S(2)}, u32[]{:S(2)}) collective-permute-start(f32[3,1,4,256]{3,1,2,0:T(1,128)S(1)} %copy.50), channel_id=1, source_target_pairs={{1,0},{2,1},{3,2},{4,3},{5,4},{6,5},{7,6},{0,7},{9,8},{10,9},{11,1... | collective-permute-start | bytes 36872 | tf_op jit(solution)/shard_map/ppermute | solution.py:94
  5.3 2.7 %shard_map.91 = f32[128,128]{1,0:T(8,128)} custom-call(f32[3,128]{1,0:T(4,128)} %pv_ref.1, f32[1,128]{1,0:T(1,128)} %bitcast.52, f32[1,128]{1,0:T(1,128)} %bitcast.53, s32[1,2048]{1,0:T(1,128)} %sp_ref.1, s32[1,128]{1,0:T(1,128)} %cnt_ref.1, f32[3,1,2048]{2,1,0:T(1,128)} %off_ref.1), custom_call_target="tpu_custom_call" | custom-call | tf_op jit(solution)/shard_map/pallas_call | solution.py:72
  7.9 9.2 %all-to-all-start = ((f32[128,1,128]{2,1,0:T(1,128)}), f32[128,1,128]{2,1,0:T(1,128)S(1)}, u32[]{:S(2)}, u32[]{:S(2)}) async-start(f32[128,1,128]{2,1,0:T(1,128)} %bitcast.46), calls=%async_computation | async-start | bytes 131072 | tf_op jit(solution)/shard_map/all_to_all | solution.py:152
  17.2 0.1 fusion.61
  17.3 0.0 copy-start.2
  17.3 0.1 fusion.62
  17.4 0.6 copy-done.2
  18.0 0.1 and_select_fusion.1
  18.2 8.8 %all-to-all-done = f32[128,1,128]{2,1,0:T(1,128)S(1)} async-done(((f32[128,1,128]{2,1,0:T(1,128)}), f32[128,1,128]{2,1,0:T(1,128)S(1)}, u32[]{:S(2)}, u32[]{:S(2)}) %all-to-all-start) | async-done | bytes 65568 | tf_op jit(solution)/shard_map/all_to_all | solution.py:152
  26.9 0.1 copy.44
  27.1 0.1 copy.47
  27.2 0.1 sub.119
  27.3 0.1 copy.48
  27.4 0.1 sub.126
  27.4 0.1 copy.46
  27.5 0.1 squeeze.4
  27.6 0.1 copy.45
  27.8 0.1 slice.83
  27.9 0.1 exponential_select_fusion
  28.1 0.1 copy.49
  28.2 0.1 sub.133
  28.3 2.1 %fusion.36 = f32[3,16,4,256]{3,1,2,0:T(8,128)S(1)} fusion(f32[3,16,4,256]{3,1,2,0:T(8,128)S(1)} %copy.63, f32[3,1,4,256]{3,1,2,0:T(1,128)S(1)} %collective-permute-done.1, f32[3,1,4,256]{3,1,2,0:T(1,128)S(1)} %collective-permute-done, f32[3,16,4,1]{3,1,2,0:T(8,128)S(1)} %get-tuple-element.14, f32[3,16,4,255]{3,1,2,0:T(8,128)S(1)} %get-tuple-element.16, ...), kind=kOutput, calls=%fused_computation.39 | convolution fusion | flops 610729984 | bytes 1392640 | tf_op jit(solution)/shard_map/dot_general | solution.py:116
  30.4 0.3 copy.64
  30.7 13.5 %all_to_all.23 = f32[6,16,4,256]{3,2,0,1:T(4,128)S(1)} all-to-all(f32[6,16,4,256]{3,2,0,1:T(4,128)S(1)} %copy.64), channel_id=1, replica_groups=mesh['gx'=16,'gy'=8] {'gx'}, dimensions={1} | all-to-all | bytes 786432 | tf_op jit(solution)/shard_map/all_to_all | solution.py:167
  44.2 0.1 slice.101
  44.3 0.1 slice.99
  44.4 0.4 convolution_bitcast_fusion
  44.8 0.1 reshape.209
  44.9 11.9 %all_to_all.24 = f32[3,16,4,256]{3,2,0,1:T(4,128)S(1)} all-to-all(f32[3,16,4,256]{3,2,0,1:T(4,128)S(1)} %copy.67), channel_id=1, replica_groups=mesh['gx'=16,'gy'=8] {'gx'}, dimensions={1} | all-to-all | bytes 393216 | tf_op jit(solution)/shard_map/all_to_all | solution.py:174
  56.8 0.7 %copy.68 = f32[3,16,4,256]{3,2,1,0:T(4,128)} copy(f32[3,16,4,256]{3,2,0,1:T(4,128)S(1)} %all_to_all.24) | data formatting | bytes 393216 | tf_op jit(solution)/shard_map/all_to_all | solution.py:174
  (27 shorter events, 0.4 us)
Async XLA Ops:
  0.0 44.4 %copy-start = (f32[64,64]{1,0:T(8,128)S(1)}, f32[64,64]{1,0:T(8,128)}, u32[]{:S(2)}) copy-start(f32[64,64]{1,0:T(8,128)} %param.17) | copy-start | bytes 49156
  0.0 17.1 %copy-start.1 = (f32[3,16,4,256]{3,2,1,0:T(4,128)S(1)}, f32[3,16,4,256]{3,2,1,0:T(4,128)}, u32[]{:S(2)}) copy-start(f32[3,16,4,256]{3,2,1,0:T(4,128)} %param.9) | copy-start | bytes 589828
  0.8 27.5 %collective-permute-start.1 = (f32[3,1,4,256]{3,1,2,0:T(1,128)S(1)}, f32[3,1,4,256]{3,1,2,0:T(1,128)S(1)}, u32[]{:S(2)}, u32[]{:S(2)}) collective-permute-start(f32[3,1,4,256]{3,1,2,0:T(1,128)S(1)} %copy.52), channel_id=1, source_target_pairs={{0,1},{1,2},{2,3},{3,4},{4,5},{5,6},{6,7},{7,0},{8,9},{9,10},{10,1... | collective-permute-start | bytes 36872 | tf_op jit(solution)/shard_map/ppermute | solution.py:91
  2.9 25.4 %collective-permute-start = (f32[3,1,4,256]{3,1,2,0:T(1,128)S(1)}, f32[3,1,4,256]{3,1,2,0:T(1,128)S(1)}, u32[]{:S(2)}, u32[]{:S(2)}) collective-permute-start(f32[3,1,4,256]{3,1,2,0:T(1,128)S(1)} %copy.50), channel_id=1, source_target_pairs={{1,0},{2,1},{3,2},{4,3},{5,4},{6,5},{7,6},{0,7},{9,8},{10,9},{11,1... | collective-permute-start | bytes 36872 | tf_op jit(solution)/shard_map/ppermute | solution.py:94
  7.9 19.0 %all-to-all-start = ((f32[128,1,128]{2,1,0:T(1,128)}), f32[128,1,128]{2,1,0:T(1,128)S(1)}, u32[]{:S(2)}, u32[]{:S(2)}) async-start(f32[128,1,128]{2,1,0:T(1,128)} %bitcast.46), calls=%async_computation | async-start | bytes 131072 | tf_op jit(solution)/shard_map/all_to_all | solution.py:152
  17.3 0.7 %copy-start.2 = (s32[1,2048]{1,0:T(1,128)S(1)}, s32[1,2048]{1,0:T(1,128)}, u32[]{:S(2)}) copy-start(s32[1,2048]{1,0:T(1,128)} %param.16) | copy-start | bytes 24580

commit v2 on v1

--- a/solution.py
+++ b/solution.py
@@ -162,13 +162,24 @@
     grad_x = (wide_x[:, 2:] - wide_x[:, :-2]) * 0.5
     grad_y = (jnp.roll(velocity, -1, axis=3) - jnp.roll(velocity, 1, axis=3)) * 0.5
     flat_part = velocity[0:1] * grad_x + velocity[1:2] * grad_y
+    inner = jnp.pad(velocity, ((0, 0), (0, 0), (1, 1), (0, 0)))
+    inner_grad_z = (inner[:, :, 2:] - inner[:, :, :-2]) * 0.5
     partial = velocity + time_step * (forcing - flat_part)
-    both = jnp.concatenate([velocity, partial], axis=0)
-    columns = lax.all_to_all(both, "gx", split_axis=1, concat_axis=2, tiled=True)
-    column_velocity = columns[0:3]
-    padded = jnp.pad(column_velocity, ((0, 0), (0, 0), (1, 1), (0, 0)))
-    grad_z = (padded[:, :, 2:] - padded[:, :, :-2]) * 0.5
-    columns = columns[3:6] - time_step * (column_velocity[2:3] * grad_z)
+    partial = partial - time_step * (velocity[2:3] * inner_grad_z)
+    half = rows_z // 2
+    edges = jnp.concatenate([velocity[:, :, :1], velocity[:, :, -1:]], axis=2)
+    packed = jnp.concatenate([partial[:, :, :half], partial[:, :, half:], edges], axis=0)
+    packed = lax.all_to_all(packed, "gx", split_axis=1, concat_axis=2, tiled=True)
+    levels = lax.axis_size("gx")
+    packed = packed.reshape(packed.shape[0], 1, levels, 2, rows_y)
+    part = jnp.concatenate([packed[0:3], packed[3:6]], axis=3)
+    edge = packed[6:9]
+    below = jnp.pad(edge[:, :, :-1, 1], ((0, 0), (0, 0), (1, 0), (0, 0)))
+    above = jnp.pad(edge[:, :, 1:, 0], ((0, 0), (0, 0), (0, 1), (0, 0)))
+    first = part[:, :, :, 0] + time_step * (edge[2:3, :, :, 0] * (below * 0.5))
+    last = part[:, :, :, -1] - time_step * (edge[2:3, :, :, 1] * (above * 0.5))
+    columns = jnp.concatenate([first[:, :, :, None], part[:, :, :, 1:-1], last[:, :, :, None]], axis=3)
+    columns = columns.reshape(3, 1, levels * rows_z, rows_y)
     solved = jnp.einsum("zk,cxky->cxzy", vertical_inverse, columns, precision=lax.Precision.HIGHEST)
     solved = solved.reshape(3, rows_x, rows_z, rows_y)
     new_velocity = lax.all_to_all(solved, "gx", split_axis=1, concat_axis=1, tiled=True)

time: 57.8 us -> 56.6 us (0.979)
  waiting for transfers between devices: 8.76 us -> 4.35 us
  blocking collectives: 25.3 us -> 27.1 us
  starting transfers between devices: 13.6 us -> 15.1 us
    all_to_all x1, waiting for transfers between devices: 8.75 us -> 4.34 us  [local(): lax.all_to_all(records, ('gx', 'gy'), split_axis=0, concat_axis=0, tiled=...]
    all_to_all x1, starting transfers between devices: 9.18 us -> 11.5 us  [local(): lax.all_to_all(records, ('gx', 'gy'), split_axis=0, concat_axis=0, tiled=...]
    ppermute x1, starting transfers between devices: 2.1 us -> 0.07 us  [with_halo(): lax.ppermute(lax.slice_in_dim(block, block.shape[dim] - width, None, axis...]
    all_to_all x1, blocking collectives: 13.5 us -> 15.4 us  [local(): lax.all_to_all(packed, 'gx', split_axis=1, concat_axis=2, tiled=True)]
    ppermute x1, starting transfers between devices: 2.37 us -> 3.54 us  [with_halo(): lax.ppermute(lax.slice_in_dim(block, 0, width, axis=dim), axis, backward)]
  transfers between devices with their start and end apart: 3 -> 3, of which waited for: 1 -> 1; matrix products, arithmetic and copies ran while one was open for 3% -> 4% of each run, Pallas kernels for 5% -> 0%
where the time goes in v2:
time: 56.6 us; the launch traced here: 56.3 us
  blocking collectives  27.1 us (48%)
  starting transfers between devices  15.1 us (27%)
  waiting for transfers between devices  4.35 us (8%)
  local copies, waits for them, and re-layouts  3.98 us (7%)
  Pallas kernels  2.69 us (5%)
  matrix products  2.39 us (4%)
    all_to_all x1, blocking collectives, local(): lax.all_to_all(packed, 'gx', split_axis=1, concat_axis=2, tiled=True)  15.4 us
    all_to_all x1, blocking collectives, local(): lax.all_to_all(solved, 'gx', split_axis=1, concat_axis=1, tiled=True)  11.6 us
    all_to_all x1, starting transfers between devices, local(): lax.all_to_all(records, ('gx', 'gy'), split_axis=0, concat_axis=0, tiled=...  11.5 us
    all_to_all x1, waiting for transfers between devices, local(): lax.all_to_all(records, ('gx', 'gy'), split_axis=0, concat_axis=0, tiled=...  4.34 us
    ppermute x1, starting transfers between devices, with_halo(): lax.ppermute(lax.slice_in_dim(block, 0, width, axis=dim), axis, backward)  3.54 us
    pallas_call x1, Pallas kernels, source_records(): pl.pallas_call(source_kernel, out_shape=jax.ShapeDtypeStruct((tiles, 8 *...  2.69 us
    dot_general x1, matrix products, deposit_blocks(): lax.dot_general(left, along_y, (((1,), (1,)), ((), ())), precision=lax.Pr...  2.07 us
  transfers between devices with their start and end apart: 3, of which 1 were waited for; matrix products, arithmetic and copies ran while one was open for 4% of the time, Pallas kernels for 0%

profile of v2, /device:TPU:1, one launch (start us, length us, event | category | flops | bytes accessed | tf_op | source)
XLA Modules:
  0.0 56.3 jit_solution(12606281524432983054)
XLA Ops:
  0.0 2.7 %shard_map.91 = f32[128,128]{1,0:T(8,128)} custom-call(f32[3,128]{1,0:T(4,128)} %pv_ref.1, f32[1,128]{1,0:T(1,128)} %bitcast.77, f32[1,128]{1,0:T(1,128)} %bitcast.78, s32[1,2048]{1,0:T(1,128)} %sp_ref.1, s32[1,128]{1,0:T(1,128)} %cnt_ref.1, f32[3,1,2048]{2,1,0:T(1,128)} %off_ref.1), custom_call_target="tpu_custom_call" | custom-call | tf_op jit(solution)/shard_map/pallas_call | solution.py:72
  2.7 11.5 %all-to-all-start = ((f32[128,1,128]{2,1,0:T(1,128)}), f32[128,1,128]{2,1,0:T(1,128)S(1)}, u32[]{:S(2)}, u32[]{:S(2)}) async-start(f32[128,1,128]{2,1,0:T(1,128)} %bitcast.71), calls=%async_computation | async-start | bytes 131072 | tf_op jit(solution)/shard_map/all_to_all | solution.py:152
  14.2 0.7 %fusion.65 = (f32[3,1,4,256]{3,2,1,0:T(4,128)S(1)}, f32[3,1,4,256]{3,2,1,0:T(4,128)S(1)}) fusion(f32[3,16,4,256]{3,2,1,0:T(4,128)} %param.9), kind=kLoop, calls=%fused_computation.100 | loop fusion | bytes 49152 | tf_op jit(solution)/shard_map/slice | solution.py:94
  14.9 3.5 %collective-permute-start = (f32[3,1,4,256]{3,1,2,0:T(1,128)S(1)}, f32[3,1,4,256]{3,1,2,0:T(1,128)S(1)}, u32[]{:S(2)}, u32[]{:S(2)}) collective-permute-start(f32[3,1,4,256]{3,1,2,0:T(1,128)S(1)} %copy.89), channel_id=1, source_target_pairs={{1,0},{2,1},{3,2},{4,3},{5,4},{6,5},{7,6},{0,7},{9,8},{10,9},{11,1... | collective-permute-start | bytes 36872 | tf_op jit(solution)/shard_map/ppermute | solution.py:94
  18.5 0.1 collective-permute-start.1
  18.6 0.1 fusion.64
  18.7 0.0 copy-start.2
  18.8 0.1 fusion.63
  18.9 0.5 copy-done.2
  19.5 0.1 and_select_fusion.1
  19.7 4.3 %all-to-all-done = f32[128,1,128]{2,1,0:T(1,128)S(1)} async-done(((f32[128,1,128]{2,1,0:T(1,128)}), f32[128,1,128]{2,1,0:T(1,128)S(1)}, u32[]{:S(2)}, u32[]{:S(2)}) %all-to-all-start) | async-done | bytes 65568 | tf_op jit(solution)/shard_map/all_to_all | solution.py:152
  24.0 0.1 copy.83
  24.1 0.1 copy.85
  24.2 0.1 squeeze.18
  24.3 0.1 copy.86
  24.4 0.1 sub.122
  24.5 0.1 copy.84
  24.6 0.1 slice.120
  24.8 0.1 copy.87
  24.9 0.1 sub.129
  25.0 0.1 exponential_select_fusion
  25.2 0.1 copy.88
  25.3 0.1 sub.136
  25.4 2.1 %fusion.28 = f32[3,16,4,256]{3,1,2,0:T(8,128)S(1)} fusion(f32[3,16,4,256]{3,1,2,0:T(8,128)S(1)} %copy.99, f32[3,1,4,256]{3,1,2,0:T(1,128)S(1)} %collective-permute-done.1, f32[3,1,4,256]{3,1,2,0:T(1,128)S(1)} %collective-permute-done, f32[3,16,4,1]{3,1,2,0:T(8,128)S(1)} %get-tuple-element.18, f32[3,16,4,255]{3,1,2,0:T(8,128)S(1)} %get-tuple-element.20, ...), kind=kOutput, calls=%fused_computation.33 | convolution fusion | flops 610926592 | bytes 1458176 | tf_op jit(solution)/shard_map/dot_general | solution.py:116
  27.5 0.2 copy.104
  27.7 15.4 %all_to_all.23 = f32[9,16,2,256]{3,2,0,1:T(2,128)S(1)} all-to-all(f32[9,16,2,256]{3,2,0,1:T(2,128)S(1)} %copy.104), channel_id=1, replica_groups=mesh['gx'=16,'gy'=8] {'gx'}, dimensions={1} | all-to-all | bytes 589824 | tf_op jit(solution)/shard_map/all_to_all | solution.py:172
  43.4 0.1 copy.108
  43.5 0.1 reshape.219
  43.6 0.3 convolution_bitcast_fusion
  43.9 0.1 reshape.220
  44.0 11.6 %all_to_all.24 = f32[3,16,4,256]{3,2,0,1:T(4,128)S(1)} all-to-all(f32[3,16,4,256]{3,2,0,1:T(4,128)S(1)} %copy.109), channel_id=1, replica_groups=mesh['gx'=16,'gy'=8] {'gx'}, dimensions={1} | all-to-all | bytes 393216 | tf_op jit(solution)/shard_map/all_to_all | solution.py:185
  55.6 0.7 %copy.110 = f32[3,16,4,256]{3,2,1,0:T(4,128)} copy(f32[3,16,4,256]{3,2,0,1:T(4,128)S(1)} %all_to_all.24) | data formatting | bytes 393216 | tf_op jit(solution)/shard_map/all_to_all | solution.py:185
  (33 shorter events, 0.5 us)
Async XLA Ops:
  0.0 43.6 %copy-start = (f32[64,64]{1,0:T(8,128)S(1)}, f32[64,64]{1,0:T(8,128)}, u32[]{:S(2)}) copy-start(f32[64,64]{1,0:T(8,128)} %param.17) | copy-start | bytes 49156
  0.0 18.6 %copy-start.1 = (f32[3,16,4,256]{3,2,1,0:T(4,128)S(1)}, f32[3,16,4,256]{3,2,1,0:T(4,128)}, u32[]{:S(2)}) copy-start(f32[3,16,4,256]{3,2,1,0:T(4,128)} %param.9) | copy-start | bytes 589828
  2.7 21.3 %all-to-all-start = ((f32[128,1,128]{2,1,0:T(1,128)}), f32[128,1,128]{2,1,0:T(1,128)S(1)}, u32[]{:S(2)}, u32[]{:S(2)}) async-start(f32[128,1,128]{2,1,0:T(1,128)} %bitcast.71), calls=%async_computation | async-start | bytes 131072 | tf_op jit(solution)/shard_map/all_to_all | solution.py:152
  14.9 10.4 %collective-permute-start = (f32[3,1,4,256]{3,1,2,0:T(1,128)S(1)}, f32[3,1,4,256]{3,1,2,0:T(1,128)S(1)}, u32[]{:S(2)}, u32[]{:S(2)}) collective-permute-start(f32[3,1,4,256]{3,1,2,0:T(1,128)S(1)} %copy.89), channel_id=1, source_target_pairs={{1,0},{2,1},{3,2},{4,3},{5,4},{6,5},{7,6},{0,7},{9,8},{10,9},{11,1... | collective-permute-start | bytes 36872 | tf_op jit(solution)/shard_map/ppermute | solution.py:94
  18.5 6.8 %collective-permute-start.1 = (f32[3,1,4,256]{3,1,2,0:T(1,128)S(1)}, f32[3,1,4,256]{3,1,2,0:T(1,128)S(1)}, u32[]{:S(2)}, u32[]{:S(2)}) collective-permute-start(f32[3,1,4,256]{3,1,2,0:T(1,128)S(1)} %copy.91), channel_id=1, source_target_pairs={{0,1},{1,2},{2,3},{3,4},{4,5},{5,6},{6,7},{7,0},{8,9},{9,10},{10,1... | collective-permute-start | bytes 36872 | tf_op jit(solution)/shard_map/ppermute | solution.py:91
  18.7 0.7 %copy-start.2 = (s32[1,2048]{1,0:T(1,128)S(1)}, s32[1,2048]{1,0:T(1,128)}, u32[]{:S(2)}) copy-start(s32[1,2048]{1,0:T(1,128)} %param.16) | copy-start | bytes 24580

commit v3 on v1

--- a/solution.py
+++ b/solution.py
@@ -24,11 +24,10 @@
 
 
 def _exact_dot(values, pick, dims):
-    total = None
-    for piece in _pieces(values):
-        term = lax.dot_general(piece, pick, dims, preferred_element_type=jnp.float32)
-        total = term if total is None else total + term
-    return total
+    rows = values.shape[0]
+    stacked = jnp.concatenate(_pieces(values), axis=0)
+    term = lax.dot_general(stacked, pick, dims, preferred_element_type=jnp.float32)
+    return (term[:rows] + term[rows : 2 * rows]) + term[2 * rows :]
 
 
 def source_kernel(pv_ref, coef_ref, width_ref, sp_ref, cnt_ref, off_ref, out_ref):
@@ -42,7 +41,7 @@
     pv = pv_ref[...]
     speed = jnp.sqrt(pv[0:1] * pv[0:1] + pv[1:2] * pv[1:2] + pv[2:3] * pv[2:3])
     force = -(coef_ref[...] * speed) * pv
-    vals = _rows([force[0:1], force[1:2], force[2:3], width_ref[...]], (8, points))
+    vals = _rows([force[0:1], force[1:2], force[2:3], width_ref[...]], (16, points))
     pick = (lax.broadcasted_iota(jnp.int32, (points, slots), 0) == sp_ref[...]).astype(jnp.bfloat16)
     picked = _exact_dot(vals, pick, plain)
     slot_at = lax.broadcasted_iota(jnp.int32, (tiles, slots), 1)

time: 57.8 us -> 57.5 us (level)
  transfers between devices with their start and end apart: 3 -> 3, of which waited for: 1 -> 1; matrix products, arithmetic and copies ran while one was open for 3% -> 3% of each run, Pallas kernels for 5% -> 4%
where the time goes in v3:
time: 57.5 us; the launch traced here: 57.1 us
  blocking collectives  25.3 us (44%)
  starting transfers between devices  13.6 us (24%)
  waiting for transfers between devices  8.76 us (15%)
  local copies, waits for them, and re-layouts  3.99 us (7%)
  matrix products  2.43 us (4%)
  Pallas kernels  2.34 us (4%)
    all_to_all x1, blocking collectives, local(): lax.all_to_all(both, 'gx', split_axis=1, concat_axis=2, tiled=True)  13.5 us
    all_to_all x1, blocking collectives, local(): lax.all_to_all(solved, 'gx', split_axis=1, concat_axis=1, tiled=True)  11.9 us
    all_to_all x1, starting transfers between devices, local(): lax.all_to_all(records, ('gx', 'gy'), split_axis=0, concat_axis=0, tiled=...  9.18 us
    all_to_all x1, waiting for transfers between devices, local(): lax.all_to_all(records, ('gx', 'gy'), split_axis=0, concat_axis=0, tiled=...  8.75 us
    ppermute x1, starting transfers between devices, with_halo(): lax.ppermute(lax.slice_in_dim(block, 0, width, axis=dim), axis, backward)  2.37 us
    pallas_call x1, Pallas kernels, source_records(): pl.pallas_call(source_kernel, out_shape=jax.ShapeDtypeStruct((tiles, 8 *...  2.34 us
    ppermute x1, starting transfers between devices, with_halo(): lax.ppermute(lax.slice_in_dim(block, block.shape[dim] - width, None, axis...  2.1 us
    dot_general x1, matrix products, deposit_blocks(): lax.dot_general(left, along_y, (((1,), (1,)), ((), ())), precision=lax.Pr...  2.06 us
  transfers between devices with their start and end apart: 3, of which 1 were waited for; matrix products, arithmetic and copies ran while one was open for 3% of the time, Pallas kernels for 4%

profile of v3, /device:TPU:1, one launch (start us, length us, event | category | flops | bytes accessed | tf_op | source)
XLA Modules:
  0.0 57.1 jit_solution(14541851614557318067)
XLA Ops:
  0.0 0.8 %fusion.63 = (f32[3,1,4,256]{3,2,1,0:T(4,128)S(1)}, f32[3,1,4,256]{3,2,1,0:T(4,128)S(1)}) fusion(f32[3,16,4,256]{3,2,1,0:T(4,128)} %param.9), kind=kLoop, calls=%fused_computation.85 | loop fusion | bytes 49152 | tf_op jit(solution)/shard_map/slice | solution.py:93
  0.8 2.1 %collective-permute-start.1 = (f32[3,1,4,256]{3,1,2,0:T(1,128)S(1)}, f32[3,1,4,256]{3,1,2,0:T(1,128)S(1)}, u32[]{:S(2)}, u32[]{:S(2)}) collective-permute-start(f32[3,1,4,256]{3,1,2,0:T(1,128)S(1)} %copy.52), channel_id=1, source_target_pairs={{0,1},{1,2},{2,3},{3,4},{4,5},{5,6},{6,7},{7,0},{8,9},{9,10},{10,1... | collective-permute-start | bytes 36872 | tf_op jit(solution)/shard_map/ppermute | solution.py:90
  2.9 2.4 %collective-permute-start = (f32[3,1,4,256]{3,1,2,0:T(1,128)S(1)}, f32[3,1,4,256]{3,1,2,0:T(1,128)S(1)}, u32[]{:S(2)}, u32[]{:S(2)}) collective-permute-start(f32[3,1,4,256]{3,1,2,0:T(1,128)S(1)} %copy.50), channel_id=1, source_target_pairs={{1,0},{2,1},{3,2},{4,3},{5,4},{6,5},{7,6},{0,7},{9,8},{10,9},{11,1... | collective-permute-start | bytes 36872 | tf_op jit(solution)/shard_map/ppermute | solution.py:93
  5.3 2.3 %shard_map.91 = f32[128,128]{1,0:T(8,128)} custom-call(f32[3,128]{1,0:T(4,128)} %pv_ref.1, f32[1,128]{1,0:T(1,128)} %bitcast.52, f32[1,128]{1,0:T(1,128)} %bitcast.53, s32[1,2048]{1,0:T(1,128)} %sp_ref.1, s32[1,128]{1,0:T(1,128)} %cnt_ref.1, f32[3,1,2048]{2,1,0:T(1,128)} %off_ref.1), custom_call_target="tpu_custom_call" | custom-call | tf_op jit(solution)/shard_map/pallas_call | solution.py:71
  7.6 9.2 %all-to-all-start = ((f32[128,1,128]{2,1,0:T(1,128)}), f32[128,1,128]{2,1,0:T(1,128)S(1)}, u32[]{:S(2)}, u32[]{:S(2)}) async-start(f32[128,1,128]{2,1,0:T(1,128)} %bitcast.46), calls=%async_computation | async-start | bytes 131072 | tf_op jit(solution)/shard_map/all_to_all | solution.py:151
  16.9 0.1 fusion.61
  17.0 0.0 copy-start.2
  17.0 0.1 fusion.62
  17.1 0.6 %copy-done.2 = s32[1,2048]{1,0:T(1,128)S(1)} copy-done((s32[1,2048]{1,0:T(1,128)S(1)}, s32[1,2048]{1,0:T(1,128)}, u32[]{:S(2)}) %copy-start.2) | copy-done | bytes 8216
  17.7 0.1 and_select_fusion.1
  17.9 8.8 %all-to-all-done = f32[128,1,128]{2,1,0:T(1,128)S(1)} async-done(((f32[128,1,128]{2,1,0:T(1,128)}), f32[128,1,128]{2,1,0:T(1,128)S(1)}, u32[]{:S(2)}, u32[]{:S(2)}) %all-to-all-start) | async-done | bytes 65568 | tf_op jit(solution)/shard_map/all_to_all | solution.py:151
  26.6 0.1 copy.44
  26.8 0.1 copy.47
  26.9 0.1 sub.119
  26.9 0.1 copy.48
  27.0 0.1 sub.126
  27.1 0.1 copy.46
  27.2 0.1 squeeze.4
  27.3 0.1 copy.45
  27.5 0.1 slice.83
  27.6 0.1 exponential_select_fusion
  27.8 0.1 copy.49
  27.9 0.1 sub.133
  28.0 2.1 %fusion.36 = f32[3,16,4,256]{3,1,2,0:T(8,128)S(1)} fusion(f32[3,16,4,256]{3,1,2,0:T(8,128)S(1)} %copy.63, f32[3,1,4,256]{3,1,2,0:T(1,128)S(1)} %collective-permute-done.1, f32[3,1,4,256]{3,1,2,0:T(1,128)S(1)} %collective-permute-done, f32[3,16,4,1]{3,1,2,0:T(8,128)S(1)} %get-tuple-element.14, f32[3,16,4,255]{3,1,2,0:T(8,128)S(1)} %get-tuple-element.16, ...), kind=kOutput, calls=%fused_computation.39 | convolution fusion | flops 610729984 | bytes 1392640 | tf_op jit(solution)/shard_map/dot_general | solution.py:115
  30.1 0.3 copy.64
  30.3 13.5 %all_to_all.23 = f32[6,16,4,256]{3,2,0,1:T(4,128)S(1)} all-to-all(f32[6,16,4,256]{3,2,0,1:T(4,128)S(1)} %copy.64), channel_id=1, replica_groups=mesh['gx'=16,'gy'=8] {'gx'}, dimensions={1} | all-to-all | bytes 786432 | tf_op jit(solution)/shard_map/all_to_all | solution.py:166
  43.9 0.1 slice.101
  44.0 0.1 slice.99
  44.1 0.4 convolution_bitcast_fusion
  44.5 0.1 reshape.209
  44.6 11.9 %all_to_all.24 = f32[3,16,4,256]{3,2,0,1:T(4,128)S(1)} all-to-all(f32[3,16,4,256]{3,2,0,1:T(4,128)S(1)} %copy.67), channel_id=1, replica_groups=mesh['gx'=16,'gy'=8] {'gx'}, dimensions={1} | all-to-all | bytes 393216 | tf_op jit(solution)/shard_map/all_to_all | solution.py:173
  56.4 0.7 %copy.68 = f32[3,16,4,256]{3,2,1,0:T(4,128)} copy(f32[3,16,4,256]{3,2,0,1:T(4,128)S(1)} %all_to_all.24) | data formatting | bytes 393216 | tf_op jit(solution)/shard_map/all_to_all | solution.py:173
  (27 shorter events, 0.4 us)
Async XLA Ops:
  0.0 44.1 %copy-start = (f32[64,64]{1,0:T(8,128)S(1)}, f32[64,64]{1,0:T(8,128)}, u32[]{:S(2)}) copy-start(f32[64,64]{1,0:T(8,128)} %param.17) | copy-start | bytes 49156
  0.0 16.8 %copy-start.1 = (f32[3,16,4,256]{3,2,1,0:T(4,128)S(1)}, f32[3,16,4,256]{3,2,1,0:T(4,128)}, u32[]{:S(2)}) copy-start(f32[3,16,4,256]{3,2,1,0:T(4,128)} %param.9) | copy-start | bytes 589828
  0.8 27.2 %collective-permute-start.1 = (f32[3,1,4,256]{3,1,2,0:T(1,128)S(1)}, f32[3,1,4,256]{3,1,2,0:T(1,128)S(1)}, u32[]{:S(2)}, u32[]{:S(2)}) collective-permute-start(f32[3,1,4,256]{3,1,2,0:T(1,128)S(1)} %copy.52), channel_id=1, source_target_pairs={{0,1},{1,2},{2,3},{3,4},{4,5},{5,6},{6,7},{7,0},{8,9},{9,10},{10,1... | collective-permute-start | bytes 36872 | tf_op jit(solution)/shard_map/ppermute | solution.py:90
  2.9 25.1 %collective-permute-start = (f32[3,1,4,256]{3,1,2,0:T(1,128)S(1)}, f32[3,1,4,256]{3,1,2,0:T(1,128)S(1)}, u32[]{:S(2)}, u32[]{:S(2)}) collective-permute-start(f32[3,1,4,256]{3,1,2,0:T(1,128)S(1)} %copy.50), channel_id=1, source_target_pairs={{1,0},{2,1},{3,2},{4,3},{5,4},{6,5},{7,6},{0,7},{9,8},{10,9},{11,1... | collective-permute-start | bytes 36872 | tf_op jit(solution)/shard_map/ppermute | solution.py:93
  7.6 19.0 %all-to-all-start = ((f32[128,1,128]{2,1,0:T(1,128)}), f32[128,1,128]{2,1,0:T(1,128)S(1)}, u32[]{:S(2)}, u32[]{:S(2)}) async-start(f32[128,1,128]{2,1,0:T(1,128)} %bitcast.46), calls=%async_computation | async-start | bytes 131072 | tf_op jit(solution)/shard_map/all_to_all | solution.py:151
  17.0 0.7 %copy-start.2 = (s32[1,2048]{1,0:T(1,128)S(1)}, s32[1,2048]{1,0:T(1,128)}, u32[]{:S(2)}) copy-start(s32[1,2048]{1,0:T(1,128)} %param.16) | copy-start | bytes 24580

commit v4 on v3

--- a/solution.py
+++ b/solution.py
@@ -41,7 +41,9 @@
     pv = pv_ref[...]
     speed = jnp.sqrt(pv[0:1] * pv[0:1] + pv[1:2] * pv[1:2] + pv[2:3] * pv[2:3])
     force = -(coef_ref[...] * speed) * pv
-    vals = _rows([force[0:1], force[1:2], force[2:3], width_ref[...]], (16, points))
+    width = width_ref[...]
+    force = force / (math.pi**1.5 * (width * width * width))
+    vals = _rows([force[0:1], force[1:2], force[2:3], 1.0 / (width * width)], (16, points))
     pick = (lax.broadcasted_iota(jnp.int32, (points, slots), 0) == sp_ref[...]).astype(jnp.bfloat16)
     picked = _exact_dot(vals, pick, plain)
     slot_at = lax.broadcasted_iota(jnp.int32, (tiles, slots), 1)
@@ -104,9 +106,8 @@
 
 
 def deposit_blocks(arrived, corner_x, corner_z, corner_y, rows_x, rows_z, rows_y, block_edge):
-    width = arrived[6]
-    inverse_square = 1.0 / (width * width)
-    scaled = arrived[0:3] / (math.pi**1.5 * width**3)[None, :]
+    inverse_square = arrived[6]
+    scaled = arrived[0:3]
     along_x = block_factor(corner_x, arrived[3], rows_x, inverse_square, block_edge)
     along_z = block_factor(corner_z, arrived[4], rows_z, inverse_square, block_edge)
     along_y = block_factor(corner_y, arrived[5], rows_y, inverse_square, block_edge)

time: 57.5 us -> 57.4 us (level)
  no operation moved by 1% of the time
where the time goes in v4:
time: 57.4 us; the launch traced here: 57.1 us
  blocking collectives  25.3 us (44%)
  starting transfers between devices  13.6 us (24%)
  waiting for transfers between devices  8.76 us (15%)
  local copies, waits for them, and re-layouts  3.99 us (7%)
  matrix products  2.43 us (4%)
  Pallas kernels  2.34 us (4%)
    all_to_all x1, blocking collectives, local(): lax.all_to_all(both, 'gx', split_axis=1, concat_axis=2, tiled=True)  13.5 us
    all_to_all x1, blocking collectives, local(): lax.all_to_all(solved, 'gx', split_axis=1, concat_axis=1, tiled=True)  11.9 us
    all_to_all x1, starting transfers between devices, local(): lax.all_to_all(records, ('gx', 'gy'), split_axis=0, concat_axis=0, tiled=...  9.18 us
    all_to_all x1, waiting for transfers between devices, local(): lax.all_to_all(records, ('gx', 'gy'), split_axis=0, concat_axis=0, tiled=...  8.75 us
    ppermute x1, starting transfers between devices, with_halo(): lax.ppermute(lax.slice_in_dim(block, 0, width, axis=dim), axis, backward)  2.37 us
    pallas_call x1, Pallas kernels, source_records(): pl.pallas_call(source_kernel, out_shape=jax.ShapeDtypeStruct((tiles, 8 *...  2.34 us
    ppermute x1, starting transfers between devices, with_halo(): lax.ppermute(lax.slice_in_dim(block, block.shape[dim] - width, None, axis...  2.1 us
    dot_general x1, matrix products, deposit_blocks(): lax.dot_general(left, along_y, (((1,), (1,)), ((), ())), precision=lax.Pr...  2.06 us
  transfers between devices with their start and end apart: 3, of which 1 were waited for; matrix products, arithmetic and copies ran while one was open for 3% of the time, Pallas kernels for 4%

profile of v4, /device:TPU:1, one launch (start us, length us, event | category | flops | bytes accessed | tf_op | source)
XLA Modules:
  0.0 57.1 jit_solution(7815228469069455761)
XLA Ops:
  0.0 0.8 %fusion.62 = (f32[3,1,4,256]{3,2,1,0:T(4,128)S(1)}, f32[3,1,4,256]{3,2,1,0:T(4,128)S(1)}) fusion(f32[3,16,4,256]{3,2,1,0:T(4,128)} %param.9), kind=kLoop, calls=%fused_computation.81 | loop fusion | bytes 49152 | tf_op jit(solution)/shard_map/slice | solution.py:95
  0.8 2.1 %collective-permute-start.1 = (f32[3,1,4,256]{3,1,2,0:T(1,128)S(1)}, f32[3,1,4,256]{3,1,2,0:T(1,128)S(1)}, u32[]{:S(2)}, u32[]{:S(2)}) collective-permute-start(f32[3,1,4,256]{3,1,2,0:T(1,128)S(1)} %copy.52), channel_id=1, source_target_pairs={{0,1},{1,2},{2,3},{3,4},{4,5},{5,6},{6,7},{7,0},{8,9},{9,10},{10,1... | collective-permute-start | bytes 36872 | tf_op jit(solution)/shard_map/ppermute | solution.py:92
  2.9 2.4 %collective-permute-start = (f32[3,1,4,256]{3,1,2,0:T(1,128)S(1)}, f32[3,1,4,256]{3,1,2,0:T(1,128)S(1)}, u32[]{:S(2)}, u32[]{:S(2)}) collective-permute-start(f32[3,1,4,256]{3,1,2,0:T(1,128)S(1)} %copy.50), channel_id=1, source_target_pairs={{1,0},{2,1},{3,2},{4,3},{5,4},{6,5},{7,6},{0,7},{9,8},{10,9},{11,1... | collective-permute-start | bytes 36872 | tf_op jit(solution)/shard_map/ppermute | solution.py:95
  5.3 2.3 %shard_map.91 = f32[128,128]{1,0:T(8,128)} custom-call(f32[3,128]{1,0:T(4,128)} %pv_ref.1, f32[1,128]{1,0:T(1,128)} %bitcast.52, f32[1,128]{1,0:T(1,128)} %bitcast.53, s32[1,2048]{1,0:T(1,128)} %sp_ref.1, s32[1,128]{1,0:T(1,128)} %cnt_ref.1, f32[3,1,2048]{2,1,0:T(1,128)} %off_ref.1), custom_call_target="tpu_custom_call" | custom-call | tf_op jit(solution)/shard_map/pallas_call | solution.py:73
  7.6 9.2 %all-to-all-start = ((f32[128,1,128]{2,1,0:T(1,128)}), f32[128,1,128]{2,1,0:T(1,128)S(1)}, u32[]{:S(2)}, u32[]{:S(2)}) async-start(f32[128,1,128]{2,1,0:T(1,128)} %bitcast.46), calls=%async_computation | async-start | bytes 131072 | tf_op jit(solution)/shard_map/all_to_all | solution.py:152
  16.9 0.1 fusion.60
  17.0 0.0 copy-start.2
  17.0 0.1 fusion.61
  17.1 0.6 %copy-done.2 = s32[1,2048]{1,0:T(1,128)S(1)} copy-done((s32[1,2048]{1,0:T(1,128)S(1)}, s32[1,2048]{1,0:T(1,128)}, u32[]{:S(2)}) %copy-start.2) | copy-done | bytes 8216
  17.7 0.1 and_select_fusion.1
  17.9 8.8 %all-to-all-done = f32[128,1,128]{2,1,0:T(1,128)S(1)} async-done(((f32[128,1,128]{2,1,0:T(1,128)}), f32[128,1,128]{2,1,0:T(1,128)S(1)}, u32[]{:S(2)}, u32[]{:S(2)}) %all-to-all-start) | async-done | bytes 65568 | tf_op jit(solution)/shard_map/all_to_all | solution.py:152
  26.6 0.1 copy.44
  26.8 0.1 copy.46
  26.9 0.1 sub.119
  26.9 0.1 copy.48
  27.0 0.1 sub.126
  27.1 0.1 copy.47
  27.2 0.1 mul.143
  27.3 0.1 copy.45
  27.4 0.1 mul.140
  27.6 0.1 exponential_select_fusion
  27.7 0.1 copy.49
  27.8 0.1 sub.133
  27.9 2.1 %fusion.36 = f32[3,16,4,256]{3,1,2,0:T(8,128)S(1)} fusion(f32[3,16,4,256]{3,1,2,0:T(8,128)S(1)} %copy.63, f32[3,1,4,256]{3,1,2,0:T(1,128)S(1)} %collective-permute-done.1, f32[3,1,4,256]{3,1,2,0:T(1,128)S(1)} %collective-permute-done, f32[3,16,4,1]{3,1,2,0:T(8,128)S(1)} %get-tuple-element.14, f32[3,16,4,255]{3,1,2,0:T(8,128)S(1)} %get-tuple-element.16, ...), kind=kOutput, calls=%fused_computation.39 | convolution fusion | flops 610729984 | bytes 1392640 | tf_op jit(solution)/shard_map/dot_general | solution.py:116
  30.0 0.3 copy.64
  30.3 13.5 %all_to_all.23 = f32[6,16,4,256]{3,2,0,1:T(4,128)S(1)} all-to-all(f32[6,16,4,256]{3,2,0,1:T(4,128)S(1)} %copy.64), channel_id=1, replica_groups=mesh['gx'=16,'gy'=8] {'gx'}, dimensions={1} | all-to-all | bytes 786432 | tf_op jit(solution)/shard_map/all_to_all | solution.py:167
  43.9 0.1 slice.98
  44.0 0.1 slice.96
  44.1 0.4 convolution_bitcast_fusion
  44.5 0.1 reshape.186
  44.5 11.9 %all_to_all.24 = f32[3,16,4,256]{3,2,0,1:T(4,128)S(1)} all-to-all(f32[3,16,4,256]{3,2,0,1:T(4,128)S(1)} %copy.67), channel_id=1, replica_groups=mesh['gx'=16,'gy'=8] {'gx'}, dimensions={1} | all-to-all | bytes 393216 | tf_op jit(solution)/shard_map/all_to_all | solution.py:174
  56.4 0.7 %copy.68 = f32[3,16,4,256]{3,2,1,0:T(4,128)} copy(f32[3,16,4,256]{3,2,0,1:T(4,128)S(1)} %all_to_all.24) | data formatting | bytes 393216 | tf_op jit(solution)/shard_map/all_to_all | solution.py:174
  (25 shorter events, 0.4 us)
Async XLA Ops:
  0.0 44.1 %copy-start = (f32[64,64]{1,0:T(8,128)S(1)}, f32[64,64]{1,0:T(8,128)}, u32[]{:S(2)}) copy-start(f32[64,64]{1,0:T(8,128)} %param.17) | copy-start | bytes 49156
  0.0 16.8 %copy-start.1 = (f32[3,16,4,256]{3,2,1,0:T(4,128)S(1)}, f32[3,16,4,256]{3,2,1,0:T(4,128)}, u32[]{:S(2)}) copy-start(f32[3,16,4,256]{3,2,1,0:T(4,128)} %param.9) | copy-start | bytes 589828
  0.8 27.1 %collective-permute-start.1 = (f32[3,1,4,256]{3,1,2,0:T(1,128)S(1)}, f32[3,1,4,256]{3,1,2,0:T(1,128)S(1)}, u32[]{:S(2)}, u32[]{:S(2)}) collective-permute-start(f32[3,1,4,256]{3,1,2,0:T(1,128)S(1)} %copy.52), channel_id=1, source_target_pairs={{0,1},{1,2},{2,3},{3,4},{4,5},{5,6},{6,7},{7,0},{8,9},{9,10},{10,1... | collective-permute-start | bytes 36872 | tf_op jit(solution)/shard_map/ppermute | solution.py:92
  2.9 25.0 %collective-permute-start = (f32[3,1,4,256]{3,1,2,0:T(1,128)S(1)}, f32[3,1,4,256]{3,1,2,0:T(1,128)S(1)}, u32[]{:S(2)}, u32[]{:S(2)}) collective-permute-start(f32[3,1,4,256]{3,1,2,0:T(1,128)S(1)} %copy.50), channel_id=1, source_target_pairs={{1,0},{2,1},{3,2},{4,3},{5,4},{6,5},{7,6},{0,7},{9,8},{10,9},{11,1... | collective-permute-start | bytes 36872 | tf_op jit(solution)/shard_map/ppermute | solution.py:95
  7.6 19.0 %all-to-all-start = ((f32[128,1,128]{2,1,0:T(1,128)}), f32[128,1,128]{2,1,0:T(1,128)S(1)}, u32[]{:S(2)}, u32[]{:S(2)}) async-start(f32[128,1,128]{2,1,0:T(1,128)} %bitcast.46), calls=%async_computation | async-start | bytes 131072 | tf_op jit(solution)/shard_map/all_to_all | solution.py:152
  17.0 0.7 %copy-start.2 = (s32[1,2048]{1,0:T(1,128)S(1)}, s32[1,2048]{1,0:T(1,128)}, u32[]{:S(2)}) copy-start(s32[1,2048]{1,0:T(1,128)} %param.16) | copy-start | bytes 24580

commit v5 on v2

--- a/solution.py
+++ b/solution.py
@@ -24,11 +24,10 @@
 
 
 def _exact_dot(values, pick, dims):
-    total = None
-    for piece in _pieces(values):
-        term = lax.dot_general(piece, pick, dims, preferred_element_type=jnp.float32)
-        total = term if total is None else total + term
-    return total
+    rows = values.shape[0]
+    stacked = jnp.concatenate(_pieces(values), axis=0)
+    term = lax.dot_general(stacked, pick, dims, preferred_element_type=jnp.float32)
+    return (term[:rows] + term[rows : 2 * rows]) + term[2 * rows :]
 
 
 def source_kernel(pv_ref, coef_ref, width_ref, sp_ref, cnt_ref, off_ref, out_ref):
@@ -42,7 +41,7 @@
     pv = pv_ref[...]
     speed = jnp.sqrt(pv[0:1] * pv[0:1] + pv[1:2] * pv[1:2] + pv[2:3] * pv[2:3])
     force = -(coef_ref[...] * speed) * pv
-    vals = _rows([force[0:1], force[1:2], force[2:3], width_ref[...]], (8, points))
+    vals = _rows([force[0:1], force[1:2], force[2:3], width_ref[...]], (16, points))
     pick = (lax.broadcasted_iota(jnp.int32, (points, slots), 0) == sp_ref[...]).astype(jnp.bfloat16)
     picked = _exact_dot(vals, pick, plain)
     slot_at = lax.broadcasted_iota(jnp.int32, (tiles, slots), 1)
@@ -166,14 +165,13 @@
     inner_grad_z = (inner[:, :, 2:] - inner[:, :, :-2]) * 0.5
     partial = velocity + time_step * (forcing - flat_part)
     partial = partial - time_step * (velocity[2:3] * inner_grad_z)
-    half = rows_z // 2
     edges = jnp.concatenate([velocity[:, :, :1], velocity[:, :, -1:]], axis=2)
-    packed = jnp.concatenate([partial[:, :, :half], partial[:, :, half:], edges], axis=0)
+    edges = edges.reshape(3, rows_x, rows_z, 2 * rows_y // rows_z)
+    packed = jnp.concatenate([partial, edges], axis=3)
     packed = lax.all_to_all(packed, "gx", split_axis=1, concat_axis=2, tiled=True)
     levels = lax.axis_size("gx")
-    packed = packed.reshape(packed.shape[0], 1, levels, 2, rows_y)
-    part = jnp.concatenate([packed[0:3], packed[3:6]], axis=3)
-    edge = packed[6:9]
+    part = packed[..., :rows_y].reshape(3, 1, levels, rows_z, rows_y)
+    edge = packed[..., rows_y:].reshape(3, 1, levels, 2, rows_y)
     below = jnp.pad(edge[:, :, :-1, 1], ((0, 0), (0, 0), (1, 0), (0, 0)))
     above = jnp.pad(edge[:, :, 1:, 0], ((0, 0), (0, 0), (0, 1), (0, 0)))
     first = part[:, :, :, 0] + time_step * (edge[2:3, :, :, 0] * (below * 0.5))

time: 56.6 us -> 56.6 us (level)
  transfers between devices with their start and end apart: 3 -> 3, of which waited for: 1 -> 1; matrix products, arithmetic and copies ran while one was open for 4% -> 5% of each run, Pallas kernels for 0% -> 0%
where the time goes in v5:
time: 56.6 us; the launch traced here: 56.3 us
  blocking collectives  27 us (48%)
  starting transfers between devices  15.1 us (27%)
  local copies, waits for them, and re-layouts  4.19 us (7%)
  waiting for transfers between devices  4.05 us (7%)
  matrix products  2.4 us (4%)
  Pallas kernels  2.38 us (4%)
  other arithmetic  0.74 us (1%)
    all_to_all x1, blocking collectives, local(): lax.all_to_all(packed, 'gx', split_axis=1, concat_axis=2, tiled=True)  15.4 us
    all_to_all x1, blocking collectives, local(): lax.all_to_all(solved, 'gx', split_axis=1, concat_axis=1, tiled=True)  11.6 us
    all_to_all x1, starting transfers between devices, local(): lax.all_to_all(records, ('gx', 'gy'), split_axis=0, concat_axis=0, tiled=...  11.5 us
    all_to_all x1, waiting for transfers between devices, local(): lax.all_to_all(records, ('gx', 'gy'), split_axis=0, concat_axis=0, tiled=...  4.04 us
    ppermute x1, starting transfers between devices, with_halo(): lax.ppermute(lax.slice_in_dim(block, 0, width, axis=dim), axis, backward)  3.54 us
    pallas_call x1, Pallas kernels, source_records(): pl.pallas_call(source_kernel, out_shape=jax.ShapeDtypeStruct((tiles, 8 *...  2.38 us
    dot_general x1, matrix products, deposit_blocks(): lax.dot_general(left, along_y, (((1,), (1,)), ((), ())), precision=lax.Pr...  2.08 us
  transfers between devices with their start and end apart: 3, of which 1 were waited for; matrix products, arithmetic and copies ran while one was open for 5% of the time, Pallas kernels for 0%

profile of v5, /device:TPU:1, one launch (start us, length us, event | category | flops | bytes accessed | tf_op | source)
XLA Modules:
  0.0 56.3 jit_solution(926012900015373324)
XLA Ops:
  0.0 2.4 %shard_map.91 = f32[128,128]{1,0:T(8,128)} custom-call(f32[3,128]{1,0:T(4,128)} %pv_ref.1, f32[1,128]{1,0:T(1,128)} %bitcast.85, f32[1,128]{1,0:T(1,128)} %bitcast.86, s32[1,2048]{1,0:T(1,128)} %sp_ref.1, s32[1,128]{1,0:T(1,128)} %cnt_ref.1, f32[3,1,2048]{2,1,0:T(1,128)} %off_ref.1), custom_call_target="tpu_custom_call" | custom-call | tf_op jit(solution)/shard_map/pallas_call | solution.py:71
  2.4 11.5 %all-to-all-start = ((f32[128,1,128]{2,1,0:T(1,128)}), f32[128,1,128]{2,1,0:T(1,128)S(1)}, u32[]{:S(2)}, u32[]{:S(2)}) async-start(f32[128,1,128]{2,1,0:T(1,128)} %bitcast.79), calls=%async_computation | async-start | bytes 131072 | tf_op jit(solution)/shard_map/all_to_all | solution.py:151
  13.9 0.7 %fusion.58 = (f32[3,1,4,256]{3,2,1,0:T(4,128)S(1)}, f32[3,1,4,256]{3,2,1,0:T(4,128)S(1)}) fusion(f32[3,16,4,256]{3,2,1,0:T(4,128)} %param.9), kind=kLoop, calls=%fused_computation.91 | loop fusion | bytes 49152 | tf_op jit(solution)/shard_map/slice | solution.py:93
  14.6 3.5 %collective-permute-start = (f32[3,1,4,256]{3,1,2,0:T(1,128)S(1)}, f32[3,1,4,256]{3,1,2,0:T(1,128)S(1)}, u32[]{:S(2)}, u32[]{:S(2)}) collective-permute-start(f32[3,1,4,256]{3,1,2,0:T(1,128)S(1)} %copy.58), channel_id=1, source_target_pairs={{1,0},{2,1},{3,2},{4,3},{5,4},{6,5},{7,6},{0,7},{9,8},{10,9},{11,1... | collective-permute-start | bytes 36872 | tf_op jit(solution)/shard_map/ppermute | solution.py:93
  18.2 0.1 collective-permute-start.1
  18.3 0.1 fusion.57
  18.4 0.1 fusion.56
  18.6 0.1 fusion.59
  18.7 0.5 copy-done.2
  19.4 0.1 pad_maximum_fusion.4
  19.5 0.1 reshape.221
  19.6 4.0 %all-to-all-done = f32[128,1,128]{2,1,0:T(1,128)S(1)} async-done(((f32[128,1,128]{2,1,0:T(1,128)}), f32[128,1,128]{2,1,0:T(1,128)S(1)}, u32[]{:S(2)}, u32[]{:S(2)}) %all-to-all-start) | async-done | bytes 65568 | tf_op jit(solution)/shard_map/all_to_all | solution.py:151
  23.7 0.1 copy.52
  23.8 0.1 copy.54
  23.9 0.1 squeeze.18
  24.0 0.1 copy.55
  24.1 0.1 sub.122
  24.2 0.1 copy.53
  24.3 0.1 slice.101
  24.5 0.1 copy.56
  24.6 0.1 sub.129
  24.8 0.1 copy.57
  24.9 0.1 sub.136
  25.0 2.1 %fusion.28 = f32[3,16,4,256]{3,1,2,0:T(8,128)S(1)} fusion(f32[3,16,4,256]{3,1,2,0:T(8,128)S(1)} %copy.68, f32[3,1,4,256]{3,1,2,0:T(1,128)S(1)} %collective-permute-done.1, f32[3,1,4,256]{3,1,2,0:T(1,128)S(1)} %collective-permute-done, f32[3,16,4,1]{3,1,2,0:T(8,128)S(1)} %get-tuple-element.15, f32[3,16,4,255]{3,1,2,0:T(8,128)S(1)} %get-tuple-element.17, ...), kind=kOutput, calls=%fused_computation.31 | convolution fusion | flops 610926592 | bytes 1458176 | tf_op jit(solution)/shard_map/dot_general | solution.py:115
  27.1 0.1 copy.72
  27.3 15.4 %all_to_all.26 = f32[3,16,4,384]{3,2,0,1:T(4,128)S(1)} all-to-all(f32[3,16,4,384]{3,2,0,1:T(4,128)S(1)} %copy.72), channel_id=1, replica_groups=mesh['gx'=16,'gy'=8] {'gx'}, dimensions={1} | all-to-all | bytes 589824 | tf_op jit(solution)/shard_map/all_to_all | solution.py:171
  42.7 0.1 all_to_all.21
  43.2 0.1 fusion.42
  43.3 0.1 pad_maximum_fusion.3
  43.6 0.3 convolution_bitcast_fusion
  44.0 11.6 %all_to_all.27 = f32[3,16,4,256]{3,2,0,1:T(4,128)S(1)} all-to-all(f32[3,16,4,256]{3,2,0,1:T(4,128)S(1)} %copy.79), channel_id=1, replica_groups=mesh['gx'=16,'gy'=8] {'gx'}, dimensions={1} | all-to-all | bytes 393216 | tf_op jit(solution)/shard_map/all_to_all | solution.py:183
  55.6 0.7 %copy.80 = f32[3,16,4,256]{3,2,1,0:T(4,128)} copy(f32[3,16,4,256]{3,2,0,1:T(4,128)S(1)} %all_to_all.27) | data formatting | bytes 393216 | tf_op jit(solution)/shard_map/all_to_all | solution.py:183
  (38 shorter events, 0.9 us)
Async XLA Ops:
  0.0 43.6 %copy-start = (f32[64,64]{1,0:T(8,128)S(1)}, f32[64,64]{1,0:T(8,128)}, u32[]{:S(2)}) copy-start(f32[64,64]{1,0:T(8,128)} %param.17) | copy-start | bytes 49156
  0.0 18.3 %copy-start.1 = (f32[3,16,4,256]{3,2,1,0:T(4,128)S(1)}, f32[3,16,4,256]{3,2,1,0:T(4,128)}, u32[]{:S(2)}) copy-start(f32[3,16,4,256]{3,2,1,0:T(4,128)} %param.9) | copy-start | bytes 589828
  2.4 21.3 %all-to-all-start = ((f32[128,1,128]{2,1,0:T(1,128)}), f32[128,1,128]{2,1,0:T(1,128)S(1)}, u32[]{:S(2)}, u32[]{:S(2)}) async-start(f32[128,1,128]{2,1,0:T(1,128)} %bitcast.79), calls=%async_computation | async-start | bytes 131072 | tf_op jit(solution)/shard_map/all_to_all | solution.py:151
  14.6 10.4 %collective-permute-start = (f32[3,1,4,256]{3,1,2,0:T(1,128)S(1)}, f32[3,1,4,256]{3,1,2,0:T(1,128)S(1)}, u32[]{:S(2)}, u32[]{:S(2)}) collective-permute-start(f32[3,1,4,256]{3,1,2,0:T(1,128)S(1)} %copy.58), channel_id=1, source_target_pairs={{1,0},{2,1},{3,2},{4,3},{5,4},{6,5},{7,6},{0,7},{9,8},{10,9},{11,1... | collective-permute-start | bytes 36872 | tf_op jit(solution)/shard_map/ppermute | solution.py:93
  18.2 6.8 %collective-permute-start.1 = (f32[3,1,4,256]{3,1,2,0:T(1,128)S(1)}, f32[3,1,4,256]{3,1,2,0:T(1,128)S(1)}, u32[]{:S(2)}, u32[]{:S(2)}) collective-permute-start(f32[3,1,4,256]{3,1,2,0:T(1,128)S(1)} %copy.60), channel_id=1, source_target_pairs={{0,1},{1,2},{2,3},{3,4},{4,5},{5,6},{6,7},{7,0},{8,9},{9,10},{10,1... | collective-permute-start | bytes 36872 | tf_op jit(solution)/shard_map/ppermute | solution.py:90
  18.5 0.7 %copy-start.2 = (s32[1,2048]{1,0:T(1,128)S(1)}, s32[1,2048]{1,0:T(1,128)}, u32[]{:S(2)}) copy-start(s32[1,2048]{1,0:T(1,128)} %param.16) | copy-start | bytes 24580

commit v6 on v3

--- a/solution.py
+++ b/solution.py
@@ -1,3 +1,4 @@
+import functools
 import math
 
 import jax
@@ -30,7 +31,7 @@
     return (term[:rows] + term[rows : 2 * rows]) + term[2 * rows :]
 
 
-def source_kernel(pv_ref, coef_ref, width_ref, sp_ref, cnt_ref, off_ref, out_ref):
+def source_kernel(pv_ref, coef_ref, width_ref, sp_ref, cnt_ref, off_ref, out_ref, *, major):
     points = pv_ref.shape[1]
     slots = sp_ref.shape[1]
     tiles = cnt_ref.shape[1]
@@ -61,15 +62,17 @@
     spread = jnp.where(same_c, spread, 0.0)
     slot_row = lax.broadcasted_iota(jnp.int32, (slots, tiles), 0)
     tile_col = lax.broadcasted_iota(jnp.int32, (slots, tiles), 1)
+    minor = tiles // major
+    tile_col = (tile_col % major) * minor + tile_col // major
     slot_tile = (slot_row // capacity == tile_col).astype(jnp.bfloat16)
     out_ref[...] = _exact_dot(spread, slot_tile, plain).T
 
 
-def source_records(pv, coef, width, sp, cnt, off):
+def source_records(pv, coef, width, sp, cnt, off, major):
     tiles = cnt.shape[1]
     capacity = sp.shape[1] // tiles
     return pl.pallas_call(
-        source_kernel,
+        functools.partial(source_kernel, major=major),
         out_shape=jax.ShapeDtypeStruct((tiles, 8 * capacity), jnp.float32),
     )(pv, coef, width, sp, cnt, off)
 
@@ -146,12 +149,14 @@
         send_point,
         send_count,
         slot_offset,
+        lax.axis_size("gx"),
     )
     fields = records.shape[1] // capacity
-    arrived = lax.all_to_all(records, ("gx", "gy"), split_axis=0, concat_axis=0, tiled=True)
+    arrived = lax.all_to_all(records, ("gy", "gx"), split_axis=0, concat_axis=0, tiled=True)
     arrived = arrived.reshape(device_count, fields, capacity).transpose(1, 0, 2)
     arrived = arrived.reshape(fields, slot_total)
-    anchors = send_anchor[0]
+    anchors = send_anchor.reshape(lax.axis_size("gx"), lax.axis_size("gy"), capacity)
+    anchors = anchors.transpose(1, 0, 2).reshape(slot_total)
     corner_x = anchors // (rows_z * rows_y)
     remainder = anchors % (rows_z * rows_y)
     corner_z = remainder // rows_y

time: 57.5 us -> 57.6 us (level)
  waiting for transfers between devices: 8.76 us -> 7.72 us
    all_to_all x1, waiting for transfers between devices: 8.75 us -> 7.72 us  [local(): lax.all_to_all(records, ('gy', 'gx'), split_axis=0, concat_axis=0, tiled=...]
    unnamed x0 -> x1, other arithmetic: none -> 0.66 us
  transfers between devices with their start and end apart: 3 -> 3, of which waited for: 1 -> 1; matrix products, arithmetic and copies ran while one was open for 3% -> 5% of each run, Pallas kernels for 4% -> 4%
where the time goes in v6:
time: 57.6 us; the launch traced here: 57.3 us
  blocking collectives  25.7 us (45%)
  starting transfers between devices  13.6 us (24%)
  waiting for transfers between devices  7.72 us (13%)
  local copies, waits for them, and re-layouts  4.16 us (7%)
  matrix products  2.42 us (4%)
  Pallas kernels  2.34 us (4%)
  other arithmetic  0.92 us (2%)
    all_to_all x1, blocking collectives, local(): lax.all_to_all(both, 'gx', split_axis=1, concat_axis=2, tiled=True)  13.9 us
    all_to_all x1, blocking collectives, local(): lax.all_to_all(solved, 'gx', split_axis=1, concat_axis=1, tiled=True)  11.9 us
    all_to_all x1, starting transfers between devices, local(): lax.all_to_all(records, ('gy', 'gx'), split_axis=0, concat_axis=0, tiled=...  9.18 us
    all_to_all x1, waiting for transfers between devices, local(): lax.all_to_all(records, ('gy', 'gx'), split_axis=0, concat_axis=0, tiled=...  7.72 us
    ppermute x1, starting transfers between devices, with_halo(): lax.ppermute(lax.slice_in_dim(block, 0, width, axis=dim), axis, backward)  2.37 us
    pallas_call x1, Pallas kernels, source_records(): pl.pallas_call(functools.partial(source_kernel, major=major), out_shape=j...  2.34 us
    ppermute x1, starting transfers between devices, with_halo(): lax.ppermute(lax.slice_in_dim(block, block.shape[dim] - width, None, axis...  2.1 us
    dot_general x1, matrix products, deposit_blocks(): lax.dot_general(left, along_y, (((1,), (1,)), ((), ())), precision=lax.Pr...  2.05 us
  transfers between devices with their start and end apart: 3, of which 1 were waited for; matrix products, arithmetic and copies ran while one was open for 5% of the time, Pallas kernels for 4%

profile of v6, /device:TPU:1, one launch (start us, length us, event | category | flops | bytes accessed | tf_op | source)
XLA Modules:
  0.0 57.3 jit_solution(3058953301993513121)
XLA Ops:
  0.0 0.8 %fusion.67 = (f32[3,1,4,256]{3,2,1,0:T(4,128)S(1)}, f32[3,1,4,256]{3,2,1,0:T(4,128)S(1)}) fusion(f32[3,16,4,256]{3,2,1,0:T(4,128)} %param.9), kind=kLoop, calls=%fused_computation.92 | loop fusion | bytes 49152 | tf_op jit(solution)/shard_map/slice | solution.py:96
  0.8 2.1 %collective-permute-start.1 = (f32[3,1,4,256]{3,1,2,0:T(1,128)S(1)}, f32[3,1,4,256]{3,1,2,0:T(1,128)S(1)}, u32[]{:S(2)}, u32[]{:S(2)}) collective-permute-start(f32[3,1,4,256]{3,1,2,0:T(1,128)S(1)} %copy.54), channel_id=1, source_target_pairs={{0,1},{1,2},{2,3},{3,4},{4,5},{5,6},{6,7},{7,0},{8,9},{9,10},{10,1... | collective-permute-start | bytes 36872 | tf_op jit(solution)/shard_map/ppermute | solution.py:93
  2.9 2.4 %collective-permute-start = (f32[3,1,4,256]{3,1,2,0:T(1,128)S(1)}, f32[3,1,4,256]{3,1,2,0:T(1,128)S(1)}, u32[]{:S(2)}, u32[]{:S(2)}) collective-permute-start(f32[3,1,4,256]{3,1,2,0:T(1,128)S(1)} %copy.52), channel_id=1, source_target_pairs={{1,0},{2,1},{3,2},{4,3},{5,4},{6,5},{7,6},{0,7},{9,8},{10,9},{11,1... | collective-permute-start | bytes 36872 | tf_op jit(solution)/shard_map/ppermute | solution.py:96
  5.3 2.3 %shard_map.91 = f32[128,128]{1,0:T(8,128)} custom-call(f32[3,128]{1,0:T(4,128)} %pv_ref.1, f32[1,128]{1,0:T(1,128)} %bitcast.50, f32[1,128]{1,0:T(1,128)} %bitcast.51, s32[1,2048]{1,0:T(1,128)} %sp_ref.1, s32[1,128]{1,0:T(1,128)} %cnt_ref.1, f32[3,1,2048]{2,1,0:T(1,128)} %off_ref.1), custom_call_target="tpu_custom_call" | custom-call | tf_op jit(solution)/shard_map/pallas_call | solution.py:74
  7.6 9.2 %all-to-all-start = ((f32[128,1,128]{2,1,0:T(1,128)}), f32[128,1,128]{2,1,0:T(1,128)S(1)}, u32[]{:S(2)}, u32[]{:S(2)}) async-start(f32[128,1,128]{2,1,0:T(1,128)} %bitcast.46), calls=%async_computation | async-start | bytes 131072 | tf_op jit(solution)/shard_map/all_to_all | solution.py:155
  16.9 0.1 fusion.65
  17.0 0.1 fusion.66
  17.1 0.5 broadcast.281
  17.7 0.7 %reduce.3 = s32[2048]{0:T(1024)S(1)} reduce(s32[1,2048]{1,0:T(1,128)S(1)} %copy-done.2, s32[]{:T(128)} %broadcast.281), dimensions={0}, to_apply=%param.16.reduce_sub_computation.3 | reduce | bytes 16388 | tf_op args[7]
  18.4 0.1 reshape.293
  18.5 0.1 reshape.294
  18.6 7.7 %all-to-all-done = f32[128,1,128]{2,1,0:T(1,128)S(1)} async-done(((f32[128,1,128]{2,1,0:T(1,128)}), f32[128,1,128]{2,1,0:T(1,128)S(1)}, u32[]{:S(2)}, u32[]{:S(2)}) %all-to-all-start) | async-done | bytes 65568 | tf_op jit(solution)/shard_map/all_to_all | solution.py:155
  26.4 0.1 copy.45
  26.5 0.1 copy.49
  26.6 0.1 sub.114
  26.7 0.1 copy.50
  26.8 0.1 sub.121
  26.8 0.1 copy.47
  26.9 0.1 squeeze.3
  27.0 0.1 copy.46
  27.2 0.1 slice.83
  27.3 0.1 exponential_select_fusion
  27.5 0.1 copy.51
  27.6 0.1 sub.127
  27.7 2.1 %fusion.36 = f32[3,16,4,256]{3,1,2,0:T(8,128)S(1)} fusion(f32[3,16,4,256]{3,1,2,0:T(8,128)S(1)} %copy.65, f32[3,1,4,256]{3,1,2,0:T(1,128)S(1)} %collective-permute-done.1, f32[3,1,4,256]{3,1,2,0:T(1,128)S(1)} %collective-permute-done, f32[3,16,4,1]{3,1,2,0:T(8,128)S(1)} %get-tuple-element.10, f32[3,16,4,255]{3,1,2,0:T(8,128)S(1)} %get-tuple-element.12, ...), kind=kOutput, calls=%fused_computation.39 | convolution fusion | flops 610729984 | bytes 1392640 | tf_op jit(solution)/shard_map/dot_general | solution.py:118
  29.8 0.3 copy.66
  30.1 13.9 %all_to_all.23 = f32[6,16,4,256]{3,2,0,1:T(4,128)S(1)} all-to-all(f32[6,16,4,256]{3,2,0,1:T(4,128)S(1)} %copy.66), channel_id=1, replica_groups=mesh['gx'=16,'gy'=8] {'gx'}, dimensions={1} | all-to-all | bytes 786432 | tf_op jit(solution)/shard_map/all_to_all | solution.py:171
  44.0 0.1 slice.101
  44.1 0.1 slice.99
  44.2 0.4 convolution_bitcast_fusion
  44.7 11.9 %all_to_all.24 = f32[3,16,4,256]{3,2,0,1:T(4,128)S(1)} all-to-all(f32[3,16,4,256]{3,2,0,1:T(4,128)S(1)} %copy.69), channel_id=1, replica_groups=mesh['gx'=16,'gy'=8] {'gx'}, dimensions={1} | all-to-all | bytes 393216 | tf_op jit(solution)/shard_map/all_to_all | solution.py:178
  56.6 0.7 %copy.70 = f32[3,16,4,256]{3,2,1,0:T(4,128)} copy(f32[3,16,4,256]{3,2,0,1:T(4,128)S(1)} %all_to_all.24) | data formatting | bytes 393216 | tf_op jit(solution)/shard_map/all_to_all | solution.py:178
  (30 shorter events, 0.5 us)
Async XLA Ops:
  0.0 44.2 %copy-start = (f32[64,64]{1,0:T(8,128)S(1)}, f32[64,64]{1,0:T(8,128)}, u32[]{:S(2)}) copy-start(f32[64,64]{1,0:T(8,128)} %param.17) | copy-start | bytes 49156
  0.0 16.8 %copy-start.1 = (f32[3,16,4,256]{3,2,1,0:T(4,128)S(1)}, f32[3,16,4,256]{3,2,1,0:T(4,128)}, u32[]{:S(2)}) copy-start(f32[3,16,4,256]{3,2,1,0:T(4,128)} %param.9) | copy-start | bytes 589828
  0.8 26.9 %collective-permute-start.1 = (f32[3,1,4,256]{3,1,2,0:T(1,128)S(1)}, f32[3,1,4,256]{3,1,2,0:T(1,128)S(1)}, u32[]{:S(2)}, u32[]{:S(2)}) collective-permute-start(f32[3,1,4,256]{3,1,2,0:T(1,128)S(1)} %copy.54), channel_id=1, source_target_pairs={{0,1},{1,2},{2,3},{3,4},{4,5},{5,6},{6,7},{7,0},{8,9},{9,10},{10,1... | collective-permute-start | bytes 36872 | tf_op jit(solution)/shard_map/ppermute | solution.py:93
  2.9 24.8 %collective-permute-start = (f32[3,1,4,256]{3,1,2,0:T(1,128)S(1)}, f32[3,1,4,256]{3,1,2,0:T(1,128)S(1)}, u32[]{:S(2)}, u32[]{:S(2)}) collective-permute-start(f32[3,1,4,256]{3,1,2,0:T(1,128)S(1)} %copy.52), channel_id=1, source_target_pairs={{1,0},{2,1},{3,2},{4,3},{5,4},{6,5},{7,6},{0,7},{9,8},{10,9},{11,1... | collective-permute-start | bytes 36872 | tf_op jit(solution)/shard_map/ppermute | solution.py:96
  7.6 18.7 %all-to-all-start = ((f32[128,1,128]{2,1,0:T(1,128)}), f32[128,1,128]{2,1,0:T(1,128)S(1)}, u32[]{:S(2)}, u32[]{:S(2)}) async-start(f32[128,1,128]{2,1,0:T(1,128)} %bitcast.46), calls=%async_computation | async-start | bytes 131072 | tf_op jit(solution)/shard_map/all_to_all | solution.py:155
  17.0 0.7 %copy-start.2 = (s32[1,2048]{1,0:T(1,128)S(1)}, s32[1,2048]{1,0:T(1,128)}, u32[]{:S(2)}) copy-start(s32[1,2048]{1,0:T(1,128)} %param.16) | copy-start | bytes 24580

commit v7 on v4

--- a/solution.py
+++ b/solution.py
@@ -98,11 +98,14 @@
 
 
 def block_factor(corner, offset, extent, inverse_square, block_edge):
-    cells = jnp.arange(extent, dtype=jnp.int32)[:, None]
-    shifted = cells - corner[None, :]
-    inside = (shifted >= 0) & (shifted < block_edge)
-    spread = shifted.astype(jnp.float32) + 0.5 - offset[None, :]
-    return jnp.where(inside, jnp.exp(-(spread * spread) * inverse_square[None, :]), 0.0)
+    steps = jnp.arange(block_edge, dtype=jnp.int32)[:, None]
+    spread = steps.astype(jnp.float32) + 0.5 - offset[None, :]
+    values = jnp.exp(-(spread * spread) * inverse_square[None, :])
+    shifted = jnp.arange(extent, dtype=jnp.int32)[:, None] - corner[None, :]
+    result = jnp.zeros((extent, corner.shape[0]), jnp.float32)
+    for step in range(block_edge):
+        result = jnp.where(shifted == step, values[step][None, :], result)
+    return result
 
 
 def deposit_blocks(arrived, corner_x, corner_z, corner_y, rows_x, rows_z, rows_y, block_edge):

time: 57.4 us -> 57.3 us (level)
  no operation moved by 1% of the time
where the time goes in v7:
time: 57.3 us; the launch traced here: 57 us
  blocking collectives  25.3 us (44%)
  starting transfers between devices  13.6 us (24%)
  waiting for transfers between devices  8.75 us (15%)
  local copies, waits for them, and re-layouts  4.06 us (7%)
  Pallas kernels  2.34 us (4%)
  matrix products  2.14 us (4%)
    all_to_all x1, blocking collectives, local(): lax.all_to_all(both, 'gx', split_axis=1, concat_axis=2, tiled=True)  13.5 us
    all_to_all x1, blocking collectives, local(): lax.all_to_all(solved, 'gx', split_axis=1, concat_axis=1, tiled=True)  11.9 us
    all_to_all x1, starting transfers between devices, local(): lax.all_to_all(records, ('gx', 'gy'), split_axis=0, concat_axis=0, tiled=...  9.18 us
    all_to_all x1, waiting for transfers between devices, local(): lax.all_to_all(records, ('gx', 'gy'), split_axis=0, concat_axis=0, tiled=...  8.74 us
    ppermute x1, starting transfers between devices, with_halo(): lax.ppermute(lax.slice_in_dim(block, 0, width, axis=dim), axis, backward)  2.37 us
    pallas_call x1, Pallas kernels, source_records(): pl.pallas_call(source_kernel, out_shape=jax.ShapeDtypeStruct((tiles, 8 *...  2.34 us
    ppermute x1, starting transfers between devices, with_halo(): lax.ppermute(lax.slice_in_dim(block, block.shape[dim] - width, None, axis...  2.1 us
    dot_general x1, matrix products, deposit_blocks(): lax.dot_general(left, along_y, (((1,), (1,)), ((), ())), precision=lax.Pr...  1.77 us
  transfers between devices with their start and end apart: 3, of which 1 were waited for; matrix products, arithmetic and copies ran while one was open for 3% of the time, Pallas kernels for 4%

profile of v7, /device:TPU:1, one launch (start us, length us, event | category | flops | bytes accessed | tf_op | source)
XLA Modules:
  0.0 57.0 jit_solution(6432999770832915787)
XLA Ops:
  0.0 0.8 %fusion.67 = (f32[3,1,4,256]{3,2,1,0:T(4,128)S(1)}, f32[3,1,4,256]{3,2,1,0:T(4,128)S(1)}) fusion(f32[3,16,4,256]{3,2,1,0:T(4,128)} %param.9), kind=kLoop, calls=%fused_computation.88 | loop fusion | bytes 49152 | tf_op jit(solution)/shard_map/slice | solution.py:95
  0.8 2.1 %collective-permute-start.1 = (f32[3,1,4,256]{3,1,2,0:T(1,128)S(1)}, f32[3,1,4,256]{3,1,2,0:T(1,128)S(1)}, u32[]{:S(2)}, u32[]{:S(2)}) collective-permute-start(f32[3,1,4,256]{3,1,2,0:T(1,128)S(1)} %copy.52), channel_id=1, source_target_pairs={{0,1},{1,2},{2,3},{3,4},{4,5},{5,6},{6,7},{7,0},{8,9},{9,10},{10,1... | collective-permute-start | bytes 36872 | tf_op jit(solution)/shard_map/ppermute | solution.py:92
  2.9 2.4 %collective-permute-start = (f32[3,1,4,256]{3,1,2,0:T(1,128)S(1)}, f32[3,1,4,256]{3,1,2,0:T(1,128)S(1)}, u32[]{:S(2)}, u32[]{:S(2)}) collective-permute-start(f32[3,1,4,256]{3,1,2,0:T(1,128)S(1)} %copy.50), channel_id=1, source_target_pairs={{1,0},{2,1},{3,2},{4,3},{5,4},{6,5},{7,6},{0,7},{9,8},{10,9},{11,1... | collective-permute-start | bytes 36872 | tf_op jit(solution)/shard_map/ppermute | solution.py:95
  5.3 2.3 %shard_map.91 = f32[128,128]{1,0:T(8,128)} custom-call(f32[3,128]{1,0:T(4,128)} %pv_ref.1, f32[1,128]{1,0:T(1,128)} %bitcast.76, f32[1,128]{1,0:T(1,128)} %bitcast.77, s32[1,2048]{1,0:T(1,128)} %sp_ref.1, s32[1,128]{1,0:T(1,128)} %cnt_ref.1, f32[3,1,2048]{2,1,0:T(1,128)} %off_ref.1), custom_call_target="tpu_custom_call" | custom-call | tf_op jit(solution)/shard_map/pallas_call | solution.py:73
  7.6 9.2 %all-to-all-start = ((f32[128,1,128]{2,1,0:T(1,128)}), f32[128,1,128]{2,1,0:T(1,128)S(1)}, u32[]{:S(2)}, u32[]{:S(2)}) async-start(f32[128,1,128]{2,1,0:T(1,128)} %bitcast.58), calls=%async_computation | async-start | bytes 131072 | tf_op jit(solution)/shard_map/all_to_all | solution.py:155
  16.9 0.1 fusion.65
  17.0 0.0 copy-start.2
  17.0 0.1 fusion.66
  17.1 0.6 %copy-done.2 = s32[1,2048]{1,0:T(1,128)S(1)} copy-done((s32[1,2048]{1,0:T(1,128)S(1)}, s32[1,2048]{1,0:T(1,128)}, u32[]{:S(2)}) %copy-start.2) | copy-done | bytes 8216
  17.8 0.1 and_select_fusion.1
  17.9 8.7 %all-to-all-done = f32[128,1,128]{2,1,0:T(1,128)S(1)} async-done(((f32[128,1,128]{2,1,0:T(1,128)}), f32[128,1,128]{2,1,0:T(1,128)S(1)}, u32[]{:S(2)}, u32[]{:S(2)}) %all-to-all-start) | async-done | bytes 65568 | tf_op jit(solution)/shard_map/all_to_all | solution.py:155
  26.6 0.1 copy.44
  26.8 0.1 copy.46
  26.9 0.1 sub.127
  26.9 0.1 copy.49
  27.0 0.1 sub.141
  27.1 0.1 copy.48
  27.2 0.1 sub.134
  27.3 0.1 copy.47
  27.4 0.1 mul.123
  27.5 0.1 copy.45
  27.6 0.1 mul.120
  27.8 0.1 multiply_exponential_fusion.2
  28.1 1.8 %fusion.38 = f32[3,16,4,256]{3,1,2,0:T(8,128)S(1)} fusion(f32[3,16,4,256]{3,1,2,0:T(8,128)S(1)} %copy.63, f32[3,1,4,256]{3,1,2,0:T(1,128)S(1)} %collective-permute-done.1, f32[3,1,4,256]{3,1,2,0:T(1,128)S(1)} %collective-permute-done, f32[3,16,4,1]{3,1,2,0:T(8,128)S(1)} %get-tuple-element.14, f32[3,16,4,255]{3,1,2,0:T(8,128)S(1)} %get-tuple-element.16, ...), kind=kOutput, calls=%fused_computation.39 | convolution fusion | flops 609681408 | bytes 1409024 | tf_op jit(solution)/shard_map/dot_general | solution.py:119
  29.9 0.3 copy.64
  30.2 13.5 %all_to_all.23 = f32[6,16,4,256]{3,2,0,1:T(4,128)S(1)} all-to-all(f32[6,16,4,256]{3,2,0,1:T(4,128)S(1)} %copy.64), channel_id=1, replica_groups=mesh['gx'=16,'gy'=8] {'gx'}, dimensions={1} | all-to-all | bytes 786432 | tf_op jit(solution)/shard_map/all_to_all | solution.py:170
  43.8 0.1 slice.158
  43.9 0.1 slice.156
  44.0 0.4 convolution_bitcast_fusion
  44.4 0.1 reshape.245
  44.4 11.9 %all_to_all.24 = f32[3,16,4,256]{3,2,0,1:T(4,128)S(1)} all-to-all(f32[3,16,4,256]{3,2,0,1:T(4,128)S(1)} %copy.67), channel_id=1, replica_groups=mesh['gx'=16,'gy'=8] {'gx'}, dimensions={1} | all-to-all | bytes 393216 | tf_op jit(solution)/shard_map/all_to_all | solution.py:177
  56.3 0.7 %copy.68 = f32[3,16,4,256]{3,2,1,0:T(4,128)} copy(f32[3,16,4,256]{3,2,0,1:T(4,128)S(1)} %all_to_all.24) | data formatting | bytes 393216 | tf_op jit(solution)/shard_map/all_to_all | solution.py:177
  (29 shorter events, 0.5 us)
Async XLA Ops:
  0.0 44.0 %copy-start = (f32[64,64]{1,0:T(8,128)S(1)}, f32[64,64]{1,0:T(8,128)}, u32[]{:S(2)}) copy-start(f32[64,64]{1,0:T(8,128)} %param.17) | copy-start | bytes 49156
  0.0 16.8 %copy-start.1 = (f32[3,16,4,256]{3,2,1,0:T(4,128)S(1)}, f32[3,16,4,256]{3,2,1,0:T(4,128)}, u32[]{:S(2)}) copy-start(f32[3,16,4,256]{3,2,1,0:T(4,128)} %param.9) | copy-start | bytes 589828
  0.8 27.3 %collective-permute-start.1 = (f32[3,1,4,256]{3,1,2,0:T(1,128)S(1)}, f32[3,1,4,256]{3,1,2,0:T(1,128)S(1)}, u32[]{:S(2)}, u32[]{:S(2)}) collective-permute-start(f32[3,1,4,256]{3,1,2,0:T(1,128)S(1)} %copy.52), channel_id=1, source_target_pairs={{0,1},{1,2},{2,3},{3,4},{4,5},{5,6},{6,7},{7,0},{8,9},{9,10},{10,1... | collective-permute-start | bytes 36872 | tf_op jit(solution)/shard_map/ppermute | solution.py:92
  2.9 25.2 %collective-permute-start = (f32[3,1,4,256]{3,1,2,0:T(1,128)S(1)}, f32[3,1,4,256]{3,1,2,0:T(1,128)S(1)}, u32[]{:S(2)}, u32[]{:S(2)}) collective-permute-start(f32[3,1,4,256]{3,1,2,0:T(1,128)S(1)} %copy.50), channel_id=1, source_target_pairs={{1,0},{2,1},{3,2},{4,3},{5,4},{6,5},{7,6},{0,7},{9,8},{10,9},{11,1... | collective-permute-start | bytes 36872 | tf_op jit(solution)/shard_map/ppermute | solution.py:95
  7.6 19.0 %all-to-all-start = ((f32[128,1,128]{2,1,0:T(1,128)}), f32[128,1,128]{2,1,0:T(1,128)S(1)}, u32[]{:S(2)}, u32[]{:S(2)}) async-start(f32[128,1,128]{2,1,0:T(1,128)} %bitcast.58), calls=%async_computation | async-start | bytes 131072 | tf_op jit(solution)/shard_map/all_to_all | solution.py:155
  17.0 0.7 %copy-start.2 = (s32[1,2048]{1,0:T(1,128)S(1)}, s32[1,2048]{1,0:T(1,128)}, u32[]{:S(2)}) copy-start(s32[1,2048]{1,0:T(1,128)} %param.16) | copy-start | bytes 24580

commit v8 on v7

--- a/solution.py
+++ b/solution.py
@@ -41,9 +41,7 @@
     pv = pv_ref[...]
     speed = jnp.sqrt(pv[0:1] * pv[0:1] + pv[1:2] * pv[1:2] + pv[2:3] * pv[2:3])
     force = -(coef_ref[...] * speed) * pv
-    width = width_ref[...]
-    force = force / (math.pi**1.5 * (width * width * width))
-    vals = _rows([force[0:1], force[1:2], force[2:3], 1.0 / (width * width)], (16, points))
+    vals = _rows([force[0:1], force[1:2], force[2:3], width_ref[...]], (16, points))
     pick = (lax.broadcasted_iota(jnp.int32, (points, slots), 0) == sp_ref[...]).astype(jnp.bfloat16)
     picked = _exact_dot(vals, pick, plain)
     slot_at = lax.broadcasted_iota(jnp.int32, (tiles, slots), 1)
@@ -109,10 +107,15 @@
 
 
 def deposit_blocks(arrived, corner_x, corner_z, corner_y, rows_x, rows_z, rows_y, block_edge):
-    inverse_square = arrived[6]
-    scaled = arrived[0:3]
+    width = arrived[6]
+    inverse_square = 1.0 / (width * width)
+    scaled = arrived[0:3] / (math.pi**1.5 * width**3)[None, :]
     along_x = block_factor(corner_x, arrived[3], rows_x, inverse_square, block_edge)
-    along_z = block_factor(corner_z, arrived[4], rows_z, inverse_square, block_edge)
+    if rows_z == block_edge:
+        levels = jnp.arange(rows_z, dtype=jnp.float32)[:, None] + 0.5 - arrived[4][None, :]
+        along_z = jnp.exp(-(levels * levels) * inverse_square[None, :])
+    else:
+        along_z = block_factor(corner_z, arrived[4], rows_z, inverse_square, block_edge)
     along_y = block_factor(corner_y, arrived[5], rows_y, inverse_square, block_edge)
     left = scaled[:, None, None, :] * along_x[None, :, None, :] * along_z[None, None, :, :]
     left = left.reshape(3 * rows_x * rows_z, -1)

time: 57.3 us -> 57.3 us (level)
  no operation moved by 1% of the time
where the time goes in v8:
time: 57.3 us; the launch traced here: 57 us
  blocking collectives  25.3 us (44%)
  starting transfers between devices  13.6 us (24%)
  waiting for transfers between devices  8.77 us (15%)
  local copies, waits for them, and re-layouts  4.04 us (7%)
  Pallas kernels  2.34 us (4%)
  matrix products  2.14 us (4%)
    all_to_all x1, blocking collectives, local(): lax.all_to_all(both, 'gx', split_axis=1, concat_axis=2, tiled=True)  13.5 us
    all_to_all x1, blocking collectives, local(): lax.all_to_all(solved, 'gx', split_axis=1, concat_axis=1, tiled=True)  11.9 us
    all_to_all x1, starting transfers between devices, local(): lax.all_to_all(records, ('gx', 'gy'), split_axis=0, concat_axis=0, tiled=...  9.18 us
    all_to_all x1, waiting for transfers between devices, local(): lax.all_to_all(records, ('gx', 'gy'), split_axis=0, concat_axis=0, tiled=...  8.76 us
    ppermute x1, starting transfers between devices, with_halo(): lax.ppermute(lax.slice_in_dim(block, 0, width, axis=dim), axis, backward)  2.37 us
    pallas_call x1, Pallas kernels, source_records(): pl.pallas_call(source_kernel, out_shape=jax.ShapeDtypeStruct((tiles, 8 *...  2.34 us
    ppermute x1, starting transfers between devices, with_halo(): lax.ppermute(lax.slice_in_dim(block, block.shape[dim] - width, None, axis...  2.1 us
    dot_general x1, matrix products, deposit_blocks(): lax.dot_general(left, along_y, (((1,), (1,)), ((), ())), precision=lax.Pr...  1.78 us
  transfers between devices with their start and end apart: 3, of which 1 were waited for; matrix products, arithmetic and copies ran while one was open for 3% of the time, Pallas kernels for 4%

profile of v8, /device:TPU:1, one launch (start us, length us, event | category | flops | bytes accessed | tf_op | source)
XLA Modules:
  0.0 57.0 jit_solution(13232464969244553879)
XLA Ops:
  0.0 0.8 %fusion.65 = (f32[3,1,4,256]{3,2,1,0:T(4,128)S(1)}, f32[3,1,4,256]{3,2,1,0:T(4,128)S(1)}) fusion(f32[3,16,4,256]{3,2,1,0:T(4,128)} %param.9), kind=kLoop, calls=%fused_computation.86 | loop fusion | bytes 49152 | tf_op jit(solution)/shard_map/slice | solution.py:93
  0.8 2.1 %collective-permute-start.1 = (f32[3,1,4,256]{3,1,2,0:T(1,128)S(1)}, f32[3,1,4,256]{3,1,2,0:T(1,128)S(1)}, u32[]{:S(2)}, u32[]{:S(2)}) collective-permute-start(f32[3,1,4,256]{3,1,2,0:T(1,128)S(1)} %copy.52), channel_id=1, source_target_pairs={{0,1},{1,2},{2,3},{3,4},{4,5},{5,6},{6,7},{7,0},{8,9},{9,10},{10,1... | collective-permute-start | bytes 36872 | tf_op jit(solution)/shard_map/ppermute | solution.py:90
  2.9 2.4 %collective-permute-start = (f32[3,1,4,256]{3,1,2,0:T(1,128)S(1)}, f32[3,1,4,256]{3,1,2,0:T(1,128)S(1)}, u32[]{:S(2)}, u32[]{:S(2)}) collective-permute-start(f32[3,1,4,256]{3,1,2,0:T(1,128)S(1)} %copy.50), channel_id=1, source_target_pairs={{1,0},{2,1},{3,2},{4,3},{5,4},{6,5},{7,6},{0,7},{9,8},{10,9},{11,1... | collective-permute-start | bytes 36872 | tf_op jit(solution)/shard_map/ppermute | solution.py:93
  5.3 2.3 %shard_map.91 = f32[128,128]{1,0:T(8,128)} custom-call(f32[3,128]{1,0:T(4,128)} %pv_ref.1, f32[1,128]{1,0:T(1,128)} %bitcast.66, f32[1,128]{1,0:T(1,128)} %bitcast.67, s32[1,2048]{1,0:T(1,128)} %sp_ref.1, s32[1,128]{1,0:T(1,128)} %cnt_ref.1, f32[3,1,2048]{2,1,0:T(1,128)} %off_ref.1), custom_call_target="tpu_custom_call" | custom-call | tf_op jit(solution)/shard_map/pallas_call | solution.py:71
  7.6 9.2 %all-to-all-start = ((f32[128,1,128]{2,1,0:T(1,128)}), f32[128,1,128]{2,1,0:T(1,128)S(1)}, u32[]{:S(2)}, u32[]{:S(2)}) async-start(f32[128,1,128]{2,1,0:T(1,128)} %bitcast.53), calls=%async_computation | async-start | bytes 131072 | tf_op jit(solution)/shard_map/all_to_all | solution.py:158
  16.9 0.1 fusion.63
  17.0 0.0 copy-start.2
  17.0 0.1 fusion.64
  17.1 0.6 %copy-done.2 = s32[1,2048]{1,0:T(1,128)S(1)} copy-done((s32[1,2048]{1,0:T(1,128)S(1)}, s32[1,2048]{1,0:T(1,128)}, u32[]{:S(2)}) %copy-start.2) | copy-done | bytes 8216
  17.9 8.8 %all-to-all-done = f32[128,1,128]{2,1,0:T(1,128)S(1)} async-done(((f32[128,1,128]{2,1,0:T(1,128)}), f32[128,1,128]{2,1,0:T(1,128)S(1)}, u32[]{:S(2)}, u32[]{:S(2)}) %all-to-all-start) | async-done | bytes 65568 | tf_op jit(solution)/shard_map/all_to_all | solution.py:158
  26.6 0.1 copy.44
  26.8 0.1 copy.47
  26.9 0.1 sub.110
  26.9 0.1 copy.49
  27.0 0.1 sub.121
  27.1 0.1 copy.48
  27.2 0.1 sub.114
  27.3 0.1 copy.46
  27.4 0.1 squeeze.4
  27.5 0.1 copy.45
  27.6 0.1 slice.107
  27.8 0.1 multiply_exponential_fusion.2
  28.1 0.0 collective-permute-done
  28.1 1.8 %fusion.38 = f32[3,16,4,256]{3,1,2,0:T(8,128)S(1)} fusion(f32[3,16,4,256]{3,1,2,0:T(8,128)S(1)} %copy.63, f32[3,1,4,256]{3,1,2,0:T(1,128)S(1)} %collective-permute-done.1, f32[3,1,4,256]{3,1,2,0:T(1,128)S(1)} %collective-permute-done, f32[3,16,4,1]{3,1,2,0:T(8,128)S(1)} %get-tuple-element.12, f32[3,16,4,255]{3,1,2,0:T(8,128)S(1)} %get-tuple-element.14, ...), kind=kOutput, calls=%fused_computation.39 | convolution fusion | flops 609681408 | bytes 1409024 | tf_op jit(solution)/shard_map/dot_general | solution.py:122
  29.9 0.3 copy.64
  30.2 13.5 %all_to_all.23 = f32[6,16,4,256]{3,2,0,1:T(4,128)S(1)} all-to-all(f32[6,16,4,256]{3,2,0,1:T(4,128)S(1)} %copy.64), channel_id=1, replica_groups=mesh['gx'=16,'gy'=8] {'gx'}, dimensions={1} | all-to-all | bytes 786432 | tf_op jit(solution)/shard_map/all_to_all | solution.py:173
  43.8 0.1 slice.133
  43.9 0.1 slice.131
  44.0 0.4 convolution_bitcast_fusion
  44.3 0.1 reshape.232
  44.4 11.9 %all_to_all.24 = f32[3,16,4,256]{3,2,0,1:T(4,128)S(1)} all-to-all(f32[3,16,4,256]{3,2,0,1:T(4,128)S(1)} %copy.67), channel_id=1, replica_groups=mesh['gx'=16,'gy'=8] {'gx'}, dimensions={1} | all-to-all | bytes 393216 | tf_op jit(solution)/shard_map/all_to_all | solution.py:180
  56.3 0.7 %copy.68 = f32[3,16,4,256]{3,2,1,0:T(4,128)} copy(f32[3,16,4,256]{3,2,0,1:T(4,128)S(1)} %all_to_all.24) | data formatting | bytes 393216 | tf_op jit(solution)/shard_map/all_to_all | solution.py:180
  (29 shorter events, 0.5 us)
Async XLA Ops:
  0.0 44.0 %copy-start = (f32[64,64]{1,0:T(8,128)S(1)}, f32[64,64]{1,0:T(8,128)}, u32[]{:S(2)}) copy-start(f32[64,64]{1,0:T(8,128)} %param.17) | copy-start | bytes 49156
  0.0 16.8 %copy-start.1 = (f32[3,16,4,256]{3,2,1,0:T(4,128)S(1)}, f32[3,16,4,256]{3,2,1,0:T(4,128)}, u32[]{:S(2)}) copy-start(f32[3,16,4,256]{3,2,1,0:T(4,128)} %param.9) | copy-start | bytes 589828
  0.8 27.3 %collective-permute-start.1 = (f32[3,1,4,256]{3,1,2,0:T(1,128)S(1)}, f32[3,1,4,256]{3,1,2,0:T(1,128)S(1)}, u32[]{:S(2)}, u32[]{:S(2)}) collective-permute-start(f32[3,1,4,256]{3,1,2,0:T(1,128)S(1)} %copy.52), channel_id=1, source_target_pairs={{0,1},{1,2},{2,3},{3,4},{4,5},{5,6},{6,7},{7,0},{8,9},{9,10},{10,1... | collective-permute-start | bytes 36872 | tf_op jit(solution)/shard_map/ppermute | solution.py:90
  2.9 25.2 %collective-permute-start = (f32[3,1,4,256]{3,1,2,0:T(1,128)S(1)}, f32[3,1,4,256]{3,1,2,0:T(1,128)S(1)}, u32[]{:S(2)}, u32[]{:S(2)}) collective-permute-start(f32[3,1,4,256]{3,1,2,0:T(1,128)S(1)} %copy.50), channel_id=1, source_target_pairs={{1,0},{2,1},{3,2},{4,3},{5,4},{6,5},{7,6},{0,7},{9,8},{10,9},{11,1... | collective-permute-start | bytes 36872 | tf_op jit(solution)/shard_map/ppermute | solution.py:93
  7.6 19.0 %all-to-all-start = ((f32[128,1,128]{2,1,0:T(1,128)}), f32[128,1,128]{2,1,0:T(1,128)S(1)}, u32[]{:S(2)}, u32[]{:S(2)}) async-start(f32[128,1,128]{2,1,0:T(1,128)} %bitcast.53), calls=%async_computation | async-start | bytes 131072 | tf_op jit(solution)/shard_map/all_to_all | solution.py:158
  17.0 0.7 %copy-start.2 = (s32[1,2048]{1,0:T(1,128)S(1)}, s32[1,2048]{1,0:T(1,128)}, u32[]{:S(2)}) copy-start(s32[1,2048]{1,0:T(1,128)} %param.16) | copy-start | bytes 24580
